TPU v7x, 128 devices: a whole 4x4x4 slice. The times are simulated.
128 devices in a mesh: fsdp: 16 (over x_hi, y, core), dp: 8 (over z, x_lo).
Axes of the slice: x: 4 (x_hi: 2, x_lo: 2; x = x_hi * 2 + x_lo), y: 4, z: 4, core: 2. Of those that a mesh axis runs over, the one named last changes fastest.
Arguments:
- hidden: bfloat16 [12288, 8192], P('fsdp', 'dp'), may hold values from -6 to 6
- combine_weight: float32 [12288], P('fsdp'), may hold values from 0.2 to 1
- down_weight: bfloat16 [4096, 2, 8192], P('fsdp', None, 'dp'), may hold values from -0.0625 to 0.0625
- cotangent: bfloat16 [12288, 4096], P('fsdp', 'dp'), may hold values from -6 to 6
- expert_rows: int32 [16, 2], P('fsdp'), may hold values from 1 to 640, as said below
- block_expert: int32 [96], P('fsdp'), may hold values from 0 to 1, as said below
- slot_token: int32 [12288], P('fsdp'), may hold values from 0 to 767, as said below
Outputs:
- expert_out: bfloat16 [12288, 4096], P('fsdp', 'dp')
- grad_hidden: bfloat16 [12288, 8192], P('fsdp', 'dp')
- grad_down: bfloat16 [4096, 2, 8192], P('fsdp', None, 'dp')
Inputs may be any that keep to these rules, and one draw needn't show every extreme that they name: `expert_rows`: row i gives the live rows of the first and the second expert in group i; the first expert's rows fill blocks from block 0 on, the second's start at the next free block, each takes ceil(rows / 128) blocks and both together at most 6; in every draw some group uses all 6 blocks. `block_expert`: within each group: 0 for the first expert's blocks, 1 for every later block; blocks past both experts' have no live rows. `slot_token`: tokens counted within the slot's group; the live slots of one expert in a group name different tokens of that group; slots that are not live hold arbitrary tokens.
All inputs are finite; a program needn't handle non-finite values.
Results may differ from a plain program's by a relative error of at most 0.014.
Values may be sent and summed in bfloat16 or wider, within the bound.
No kernel may reach another device: no remote copies, remote signals or barrier semaphores. Data moves between devices by JAX's collectives and lax.ppermute only.
A program may use at most 192 MiB of HBM per device.

v0:
```python
import math

import jax
import jax.numpy as jnp
from jax import lax
from jax.sharding import PartitionSpec as P

EXPERTS = 2
BLK = 128


def local(hidden, combine_weight, down_weight, cotangent, expert_rows, block_expert, slot_token):
    slot_count = hidden.shape[0]
    hidden_width = hidden.shape[1]
    block_count = block_expert.shape[0]
    positions = jnp.arange(slot_count, dtype=jnp.int32)
    blocks = positions // BLK
    live_rows = expert_rows[0]
    first_blocks = (live_rows[0] + BLK - 1) // BLK
    second_blocks = (live_rows[1] + BLK - 1) // BLK
    live = jnp.where(
        blocks < first_blocks,
        positions < live_rows[0],
        (blocks < first_blocks + second_blocks) & (positions - first_blocks * BLK < live_rows[1]),
    )
    slot_scale = combine_weight * live.astype(jnp.float32)
    full_cot = lax.all_gather(cotangent, "dp", axis=1, tiled=True)
    model_width = full_cot.shape[1]
    slot_cot = (slot_scale[:, None] * full_cot[slot_token].astype(jnp.float32)).astype(jnp.bfloat16)
    hid_blocks = hidden.reshape(block_count, BLK, hidden_width)
    cot_blocks = slot_cot.reshape(block_count, BLK, model_width)
    panel = lax.all_gather(down_weight, "fsdp", axis=0, tiled=True)
    extent = panel.shape[0]

    def per_block(carry, inputs):
        hid_block, cot_block, expert = inputs
        weight = lax.dynamic_index_in_dim(panel, expert, 1, keepdims=False)
        out_block = jnp.einsum("th,ch->tc", hid_block, weight, preferred_element_type=jnp.float32)
        grad_block = jnp.einsum("tc,ch->th", cot_block, weight, preferred_element_type=jnp.float32)
        return (carry, (out_block, grad_block))

    unused, (out_piece, grad_piece) = lax.scan(per_block, 0, (hid_blocks, cot_blocks, block_expert))
    slot_out = out_piece.reshape(slot_count, extent)
    slot_out, hidden_grad = (slot_out, grad_piece.reshape(slot_count, hidden_width))
    token_count = cotangent.shape[0]
    combined = (
        jnp.zeros((token_count, model_width), jnp.float32)
        .at[slot_token]
        .add(slot_scale[:, None] * slot_out)
    )
    expert_out = lax.psum_scatter(
        combined.astype(jnp.bfloat16), "dp", scatter_dimension=1, tiled=True
    )
    block_marks = (block_expert[:, None] == jnp.arange(EXPERTS, dtype=jnp.int32)[None, :]).astype(
        jnp.bfloat16
    )
    slot_marks = jnp.repeat(block_marks, BLK, axis=0)
    masked = slot_marks[:, :, None] * slot_cot[:, None, :]
    summed = lax.psum_scatter(
        jnp.einsum("sec,sh->ceh", masked, hidden, preferred_element_type=jnp.float32).astype(
            jnp.bfloat16
        ),
        "fsdp",
        scatter_dimension=0,
        tiled=True,
    ).astype(jnp.float32)
    grad_scale = 1.0 / math.sqrt(lax.axis_size("fsdp") * slot_count)
    grad_down = (summed * grad_scale).astype(jnp.bfloat16)
    return (expert_out, hidden_grad.astype(jnp.bfloat16), grad_down)


def solution(mesh):
    in_specs = (
        P("fsdp", "dp"),
        P("fsdp"),
        P("fsdp", None, "dp"),
        P("fsdp", "dp"),
        P("fsdp", None),
        P("fsdp"),
        P("fsdp"),
    )
    out_specs = (P("fsdp", "dp"), P("fsdp", "dp"), P("fsdp", None, "dp"))
    return jax.shard_map(local, mesh=mesh, in_specs=in_specs, out_specs=out_specs, check_vma=False)
```

profile of v0, /device:TPU:1, one launch (start us, length us, event | category | flops | bytes accessed | tf_op | source)
XLA Modules:
  0.0 673.5 jit_solution(6814083249735016535)
XLA Ops:
  7.2 0.0 all-gather.5.cloned.1.call-start
  7.2 0.7 all-gather.5.cloned.1.call-update
  7.9 0.0 all-gather.3.cloned.1.call-start
  7.9 2.5 copy.12
  10.4 0.0 all-gather.3.cloned.1.call-update
  10.4 0.0 reduce-scatter.5.cloned.1.call-start
  10.5 1.3 fusion.41
  13.0 0.7 compare_convert_fusion
  13.7 0.1 broadcast_bitcast_fusion
  13.8 0.7 compare_select_fusion
  14.5 1.9 fusion.42
  16.4 1.9 fusion.38
  18.3 123.9 %all-gather.5.cloned.1.call-done = bf16[768,4096]{1,0:T(8,128)(2,1)} async-done(((bf16[768,512]{1,0:T(8,128)(2,1)}), bf16[768,4096]{1,0:T(8,128)(2,1)}) %all-gather.5.cloned.1.call-update) | async-done | bytes 6291472 | tf_op jit(solution)/shard_map/all_gather | solution.py:27
  142.2 15.6 %gather_fusion = bf16[768,4096]{1,0:T(8,128)(2,1)} fusion(bf16[768,4096]{1,0:T(8,128)(2,1)} %all-gather.5.cloned.1.call-done, s32[1024]{0:T(1024)S(1)} %pad_clamp_fusion), kind=kCustom, calls=%fused_computation | custom fusion | bytes 12585984 | tf_op jit(solution)/shard_map/gather | solution.py:29
  157.8 8.0 %multiply_convert_fusion.1 = bf16[6,128,4096]{2,1,0:T(8,128)(2,1)} fusion(f32[6,128]{1,0:T(8,128)S(1)} %fusion.42, bf16[6,128,4096]{2,1,0:T(8,128)(2,1)} %bitcast.64), kind=kLoop, calls=%fused_computation.23 | loop fusion | flops 9437184 | bytes 12585984 | tf_op jit(solution)/shard_map/convert_element_type | solution.py:29
  165.7 89.9 %all-gather.3.cloned.1.call-done = bf16[4096,2,1024]{2,0,1:T(8,128)(2,1)} async-done(((bf16[256,2,1024]{2,0,1:T(8,128)(2,1)}), bf16[4096,2,1024]{2,0,1:T(8,128)(2,1)}) %all-gather.3.cloned.1.call-update) | async-done | bytes 16777232 | tf_op jit(solution)/shard_map/all_gather | solution.py:32
  255.6 0.0 copy-done.1
  255.6 94.9 %while.12 = (s32[]{:T(128)}, f32[6,128,4096]{2,1,0:T(8,128)}, bf16[6,128,1024]{2,1,0:T(8,128)(2,1)}, bf16[6,128,1024]{2,1,0:T(8,128)(2,1)S(1)}, s32[6]{0:T(128)S...) while((s32[]{:T(128)}, f32[6,128,4096]{2,1,0:T(8,128)}, ...), condition=%wide.region_1.2_spmd, body=%wide.region_0.1_spmd.sunk | while | flops 2147483648 | bytes 20711580 | solution.py:42
  255.6 0.6 dynamic_slice.49
  258.2 7.6 %fusion.53 = f32[6,128,4096]{2,1,0:T(8,128)} fusion(f32[6,128,4096]{2,1,0:T(8,128)} %get-tuple-element.121, s32[]{:T(128)} %get-tuple-element.120, bf16[4096,2,1024]{2,0,1:T(8,128)(2,1)} %get-tuple-element.135, s32[]{:T(128)S(6)} %select_n.50, bf16[6,128,1024]{2,1,0:T(8,128)(2,1)S(1)} %get-tuple-element.133), kind=kOutput, calls=%fused_computation.9.clone.1 | convolution fusion | flops 1073741824 | bytes 10748932 | tf_op jit(solution)/shard_map/while/body/eval_jaxpr/th,ch->tc/dot_general | solution.py:38
  265.8 5.7 fusion.54
  271.5 0.6 dynamic_slice.49
  274.0 7.6 %fusion.53 = f32[6,128,4096]{2,1,0:T(8,128)} fusion(f32[6,128,4096]{2,1,0:T(8,128)} %get-tuple-element.121, s32[]{:T(128)} %get-tuple-element.120, bf16[4096,2,1024]{2,0,1:T(8,128)(2,1)} %get-tuple-element.135, s32[]{:T(128)S(6)} %select_n.50, bf16[6,128,1024]{2,1,0:T(8,128)(2,1)S(1)} %get-tuple-element.133), kind=kOutput, calls=%fused_computation.9.clone.1 | convolution fusion | flops 1073741824 | bytes 10748932 | tf_op jit(solution)/shard_map/while/body/eval_jaxpr/th,ch->tc/dot_general | solution.py:38
  281.5 5.7 fusion.54
  287.3 0.6 dynamic_slice.49
  289.8 7.6 %fusion.53 = f32[6,128,4096]{2,1,0:T(8,128)} fusion(f32[6,128,4096]{2,1,0:T(8,128)} %get-tuple-element.121, s32[]{:T(128)} %get-tuple-element.120, bf16[4096,2,1024]{2,0,1:T(8,128)(2,1)} %get-tuple-element.135, s32[]{:T(128)S(6)} %select_n.50, bf16[6,128,1024]{2,1,0:T(8,128)(2,1)S(1)} %get-tuple-element.133), kind=kOutput, calls=%fused_computation.9.clone.1 | convolution fusion | flops 1073741824 | bytes 10748932 | tf_op jit(solution)/shard_map/while/body/eval_jaxpr/th,ch->tc/dot_general | solution.py:38
  297.4 5.7 fusion.54
  303.1 0.6 dynamic_slice.49
  305.6 7.6 %fusion.53 = f32[6,128,4096]{2,1,0:T(8,128)} fusion(f32[6,128,4096]{2,1,0:T(8,128)} %get-tuple-element.121, s32[]{:T(128)} %get-tuple-element.120, bf16[4096,2,1024]{2,0,1:T(8,128)(2,1)} %get-tuple-element.135, s32[]{:T(128)S(6)} %select_n.50, bf16[6,128,1024]{2,1,0:T(8,128)(2,1)S(1)} %get-tuple-element.133), kind=kOutput, calls=%fused_computation.9.clone.1 | convolution fusion | flops 1073741824 | bytes 10748932 | tf_op jit(solution)/shard_map/while/body/eval_jaxpr/th,ch->tc/dot_general | solution.py:38
  313.2 5.7 fusion.54
  318.9 0.6 dynamic_slice.49
  321.4 7.6 %fusion.53 = f32[6,128,4096]{2,1,0:T(8,128)} fusion(f32[6,128,4096]{2,1,0:T(8,128)} %get-tuple-element.121, s32[]{:T(128)} %get-tuple-element.120, bf16[4096,2,1024]{2,0,1:T(8,128)(2,1)} %get-tuple-element.135, s32[]{:T(128)S(6)} %select_n.50, bf16[6,128,1024]{2,1,0:T(8,128)(2,1)S(1)} %get-tuple-element.133), kind=kOutput, calls=%fused_computation.9.clone.1 | convolution fusion | flops 1073741824 | bytes 10748932 | tf_op jit(solution)/shard_map/while/body/eval_jaxpr/th,ch->tc/dot_general | solution.py:38
  329.0 5.7 fusion.54
  334.7 0.6 dynamic_slice.49
  337.2 7.6 %fusion.53 = f32[6,128,4096]{2,1,0:T(8,128)} fusion(f32[6,128,4096]{2,1,0:T(8,128)} %get-tuple-element.121, s32[]{:T(128)} %get-tuple-element.120, bf16[4096,2,1024]{2,0,1:T(8,128)(2,1)} %get-tuple-element.135, s32[]{:T(128)S(6)} %select_n.50, bf16[6,128,1024]{2,1,0:T(8,128)(2,1)S(1)} %get-tuple-element.133), kind=kOutput, calls=%fused_computation.9.clone.1 | convolution fusion | flops 1073741824 | bytes 10748932 | tf_op jit(solution)/shard_map/while/body/eval_jaxpr/th,ch->tc/dot_general | solution.py:38
  344.8 5.7 fusion.54
  350.5 14.9 %multiply_convert_fusion = (bf16[768,4096]{1,0:T(8,128)(2,1)}, f32[768,4096]{1,0:T(8,128)}) fusion(f32[768]{0:T(1024)S(1)} %fusion.38, bf16[768,4096]{1,0:T(8,128)(2,1)} %gather_fusion, f32[6,128,4096]{2,1,0:T(8,128)} %get-tuple-element.41), kind=kLoop, calls=%fused_computation.22 | loop fusion | flops 12582912 | bytes 37751808 | tf_op jit(solution)/shard_map/convert_element_type | solution.py:29
  365.5 8.7 %copy.13 = bf16[768,4096]{0,1:T(8,128)(2,1)} copy(bf16[768,4096]{1,0:T(8,128)(2,1)} %get-tuple-element.63) | data formatting | bytes 12582912 | tf_op jit(solution)/shard_map/convert_element_type | solution.py:29
  374.1 17.7 %convert_bitcast_fusion = bf16[4096,2,1024]{2,0,1:T(8,128)(2,1)} fusion(bf16[768,4096]{0,1:T(8,128)(2,1)} %copy.13, bf16[768,2]{0,1:T(2,128)(2,1)S(1)} %bitcast.65, bf16[768,1024]{1,0:T(8,128)(2,1)S(1)} %bitcast.67), kind=kOutput, calls=%fused_computation.18 | convolution fusion | flops 12899581952 | bytes 24644608 | tf_op jit(solution)/shard_map/sec,sh->ceh/dot_general | solution.py:60
  391.8 0.0 reduce-scatter.5.cloned.1.call-update
  391.9 0.0 reduce-scatter.3.cloned.1.call-start
  391.9 32.3 %scatter_custom_fusion = f32[768,4096]{1,0:T(8,128)} fusion(s32[768]{0:T(1024)S(1)} %compare_select_fusion, f32[768,4096]{1,0:T(8,128)} %get-tuple-element.64, f32[]{:T(128)} %constant.60.clone.1), kind=kCustom, calls=%fused_computation.26 | custom fusion | flops 3145728 | bytes 12583424 | tf_op jit(solution)/shard_map/scatter-add | solution.py:49
  424.2 8.4 %convert_element_type.51 = bf16[768,4096]{1,0:T(8,128)(2,1)} convert(f32[768,4096]{1,0:T(8,128)} %scatter_custom_fusion) | non-fusion elementwise | flops 3145728 | bytes 18874368 | tf_op jit(solution)/shard_map/convert_element_type | solution.py:52
  432.5 0.0 reduce-scatter.3.cloned.1.call-update
  432.6 103.0 %reduce-scatter.5.cloned.1.call-done = bf16[256,2,1024]{2,0,1:T(8,128)(2,1)} async-done(((bf16[4096,2,1024]{2,0,1:T(8,128)(2,1)}), bf16[256,2,1024]{2,0,1:T(8,128)(2,1)}) %reduce-scatter.5.cloned.1.call-update) | async-done | bytes 1048592 | tf_op jit(solution)/shard_map/reduce_scatter | solution.py:59
  535.5 1.4 multiply_convert_fusion.2
  537.0 2.0 copy.14
  539.0 127.9 %reduce-scatter.3.cloned.1.call-done = bf16[768,512]{1,0:T(8,128)(2,1)} async-done(((bf16[768,4096]{1,0:T(8,128)(2,1)}), bf16[768,512]{1,0:T(8,128)(2,1)}) %reduce-scatter.3.cloned.1.call-update) | async-done | bytes 786448 | tf_op jit(solution)/shard_map/reduce_scatter | solution.py:51
  (7 shorter events, 0.0 us)
Async XLA Ops:
  7.2 135.0 %all-gather.5.cloned.1.call-start = ((), (), s32[]{:S(2)}) async-start(), calls=%async_computation.3 | async-start | bytes 7077888 | tf_op jit(solution)/shard_map/all_gather | solution.py:27
  7.9 247.7 %all-gather.3.cloned.1.call-start = ((), (), s32[]{:S(2)}) async-start(), calls=%async_computation.2 | async-start | bytes 17825792 | tf_op jit(solution)/shard_map/all_gather | solution.py:32
  10.4 525.1 %reduce-scatter.5.cloned.1.call-start = ((), (), s32[]{:S(2)}) async-start(), calls=%async_computation.5 | async-start | bytes 17825792 | tf_op jit(solution)/shard_map/reduce_scatter | solution.py:59
  157.8 97.9 %copy-start = (bf16[768,1024]{1,0:T(8,128)(2,1)S(1)}, bf16[768,1024]{1,0:T(8,128)(2,1)}, u32[]{:S(2)}) copy-start(bf16[768,1024]{1,0:T(8,128)(2,1)} %param.9) | copy-start | bytes 4718596
  157.8 97.9 %copy-start.1 = (s32[6]{0:T(128)S(1)}, s32[6]{0:T(128)}, u32[]{:S(2)}) copy-start(s32[6]{0:T(128)} %param.14) | copy-start | bytes 76
  391.9 275.1 %reduce-scatter.3.cloned.1.call-start = ((), (), s32[]{:S(2)}) async-start(), calls=%async_computation.4 | async-start | bytes 7077888 | tf_op jit(solution)/shard_map/reduce_scatter | solution.py:51
Sparse Core Ops, SparseCore 0:
  9.6 132.4 all-gather.4
  145.3 110.3 all-gather.2
  392.0 143.4 reduce-scatter.4
  538.4 128.5 reduce-scatter.2
where the time goes:
time: 675 us; the launch traced here: 673 us
  waiting for transfers between devices  445 us (66%)
  matrix products  97.4 us (14%)
  other arithmetic  70.1 us (10%)
  local copies, waits for them, and re-layouts  33.6 us (5%)
  between operations  15.1 us (2%)
  loops' own time  11.7 us (2%)
    reduce_scatter x1, waiting for transfers between devices, local(): lax.psum_scatter(combined.astype(jnp.bfloat16), 'dp', scatter_dimension=1...  128 us
    all_gather x1, waiting for transfers between devices, local(): full_cot = lax.all_gather(cotangent, 'dp', axis=1, tiled=True)  124 us
    reduce_scatter x1, waiting for transfers between devices, local(): lax.psum_scatter(jnp.einsum('sec,sh->ceh', masked, hidden, preferred_elem...  103 us
    all_gather x1, waiting for transfers between devices, local(): panel = lax.all_gather(down_weight, 'fsdp', axis=0, tiled=True)  89.9 us
    dot_general x6, matrix products, per_block(): jnp.einsum('th,ch->tc', hid_block, weight, preferred_element_type=jnp.flo...  45.6 us
    dot_general x6, matrix products, per_block(): jnp.einsum('tc,ch->th', cot_block, weight, preferred_element_type=jnp.flo...  34.1 us
    scatter-add x1, other arithmetic, local(): combined = jnp.zeros((token_count, model_width), jnp.float32).at[slot_tok...  32.3 us
    convert_element_type x2, other arithmetic, local(): (slot_scale[:, None] * full_cot[slot_token].astype(jnp.float32)).astype(j...  22.9 us
  transfers between devices with their start and end apart: 4, of which 4 were waited for; matrix products, arithmetic and copies ran while one was open for 11% of the time, Pallas kernels for 0%

commit v1 on v0

v1 whole, which is shorter than its diff:
```python
import math

import jax
import jax.numpy as jnp
from jax import lax
from jax.sharding import PartitionSpec as P

EXPERTS = 2
BLK = 128


def ring_pairs(n, k):
    return [(i, (i + k) % n) for i in range(n)]


def gather_dp(piece, axis_name):
    n = lax.axis_size(axis_name)
    me = lax.axis_index(axis_name)
    recv = [piece] + [lax.ppermute(piece, axis_name, ring_pairs(n, k)) for k in range(1, n)]
    arr = jnp.stack([recv[(-m) % n] for m in range(n)], axis=1)
    arr2 = jnp.concatenate([arr, arr], axis=1)
    return lax.dynamic_slice_in_dim(arr2, (n - me) % n, n, axis=1)


def scatter_sum_dp(full, axis_name):
    n = lax.axis_size(axis_name)
    me = lax.axis_index(axis_name)
    total = lax.dynamic_index_in_dim(full, me, axis=1, keepdims=False).astype(jnp.float32)
    for k in range(1, n):
        piece = lax.dynamic_index_in_dim(full, (me + k) % n, axis=1, keepdims=False)
        total = total + lax.ppermute(piece, axis_name, ring_pairs(n, k)).astype(jnp.float32)
    return total.astype(jnp.bfloat16)


def local(hidden, combine_weight, down_weight, cotangent, expert_rows, block_expert, slot_token):
    slot_count, hidden_width = hidden.shape
    block_count = block_expert.shape[0]
    n_dp = lax.axis_size("dp")
    positions = jnp.arange(slot_count, dtype=jnp.int32)
    blocks = positions // BLK
    live_rows = expert_rows[0]
    first_blocks = (live_rows[0] + BLK - 1) // BLK
    second_blocks = (live_rows[1] + BLK - 1) // BLK
    live = jnp.where(
        blocks < first_blocks,
        positions < live_rows[0],
        (blocks < first_blocks + second_blocks) & (positions - first_blocks * BLK < live_rows[1]),
    )
    slot_scale = combine_weight * live.astype(jnp.float32)
    slot_expert = jnp.repeat(block_expert, BLK)

    panel = lax.all_gather(jnp.transpose(down_weight, (1, 0, 2)), "fsdp", axis=1, tiled=True)
    model_width = panel.shape[1]

    full_cot = gather_dp(cotangent, "dp").reshape(slot_count, model_width)
    tok_hot = (slot_token[:, None] == positions[None, :]).astype(jnp.bfloat16)
    picked = jnp.dot(tok_hot, full_cot, preferred_element_type=jnp.float32)
    slot_cot = (slot_scale[:, None] * picked).astype(jnp.bfloat16)

    lo = (block_count - 1) * BLK
    masks = [slot_expert == e for e in range(EXPERTS)]
    windows = [(0, lo), (BLK, slot_count)]

    grads = []
    for e in range(EXPERTS):
        a, b = windows[e]
        cot_e = jnp.where(masks[e][a:b, None], slot_cot[a:b], jnp.zeros_like(slot_cot[a:b]))
        grads.append(
            jnp.einsum("sd,sh->dh", cot_e, hidden[a:b], preferred_element_type=jnp.float32).astype(
                jnp.bfloat16
            )
        )
    device_grad = jnp.stack(grads, axis=0)
    summed = lax.psum_scatter(device_grad, "fsdp", scatter_dimension=1, tiled=True).astype(
        jnp.float32
    )
    grad_scale = 1.0 / math.sqrt(lax.axis_size("fsdp") * slot_count)
    grad_down = jnp.transpose((summed * grad_scale).astype(jnp.bfloat16), (1, 0, 2))

    combined = None
    for e in range(EXPERTS):
        valid = live & masks[e]
        target = jnp.where(valid, slot_token, slot_count)
        inv = jnp.zeros((slot_count,), jnp.int32).at[target].set(positions, mode="drop")
        has = jnp.zeros((slot_count,), jnp.bool_).at[target].set(True, mode="drop")
        scale_e = jnp.where(has, slot_scale[inv], 0.0)
        sel = ((inv[:, None] == positions[None, :]) & has[:, None]).astype(jnp.bfloat16)
        hid_e = jnp.dot(sel, hidden, preferred_element_type=jnp.float32).astype(jnp.bfloat16)
        out_e = jnp.einsum("th,dh->td", hid_e, panel[e], preferred_element_type=jnp.float32)
        term = scale_e[:, None] * out_e
        combined = term if combined is None else combined + term
    token_part = combined.astype(jnp.bfloat16).reshape(slot_count, n_dp, model_width // n_dp)
    expert_out = scatter_sum_dp(token_part, "dp")

    gh = []
    for e in range(EXPERTS):
        a, b = windows[e]
        gh.append(jnp.dot(slot_cot[a:b], panel[e], preferred_element_type=jnp.float32))
    head = gh[0][:BLK]
    mid = jnp.where(masks[0][BLK:lo, None], gh[0][BLK:lo], gh[1][: lo - BLK])
    tail = gh[1][lo - BLK :]
    hidden_grad = jnp.concatenate([head, mid, tail], axis=0).astype(jnp.bfloat16)
    return (expert_out, hidden_grad, grad_down)


def solution(mesh):
    in_specs = (
        P("fsdp", "dp"),
        P("fsdp"),
        P("fsdp", None, "dp"),
        P("fsdp", "dp"),
        P("fsdp", None),
        P("fsdp"),
        P("fsdp"),
    )
    out_specs = (P("fsdp", "dp"), P("fsdp", "dp"), P("fsdp", None, "dp"))
    return jax.shard_map(local, mesh=mesh, in_specs=in_specs, out_specs=out_specs, check_vma=False)
```

time: 675 us -> 545 us (0.81)
  waiting for transfers between devices: 445 us -> 328 us
  other arithmetic: 70.1 us -> 14.2 us
  local copies, waits for them, and re-layouts: 33.6 us -> 78.3 us
  starting transfers between devices: 0.16 us -> 36.6 us
  matrix products: 97.4 us -> 67.6 us
  loops' own time: 11.7 us -> 0 us
    reduce_scatter x2 -> x1, waiting for transfers between devices: 231 us -> 123 us  [local(): lax.psum_scatter(device_grad, 'fsdp', scatter_dimension=1, tiled=True)]
    all_gather x2 -> x1, waiting for transfers between devices: 214 us -> 108 us  [local(): lax.all_gather(jnp.transpose(down_weight, (1, 0, 2)), 'fsdp', axis=1, til...]
    ppermute x0 -> x14, waiting for transfers between devices: none -> 96.9 us  [the longest x7 54 us: gather_dp(): lax.ppermute(piece, axis_name, ring_pairs(n, k))]
    ppermute x0 -> x14, starting transfers between devices: none -> 36.5 us  [the longest x7 24.8 us: gather_dp(): lax.ppermute(piece, axis_name, ring_pairs(n, k))]
    unnamed x8 -> x44, local copies, waits for them, and re-layouts: 4.61 us -> 37.5 us
    scatter-add x1 -> x0, other arithmetic: 32.3 us -> none  [local(): combined = jnp.zeros((token_count, model_width), jnp.float32).at[slot_tok...]
    convert_element_type x5 -> x1, other arithmetic: 33.4 us -> 1.8 us  [scatter_sum_dp(): return total.astype(jnp.bfloat16)]
    dot_general x13 -> x7, matrix products: 97.4 us -> 67.6 us  [the longest x2 29.8 us: local(): jnp.einsum('th,dh->td', hid_e, panel[e], preferred_element_type=jnp.float32)]
  transfers between devices with their start and end apart: 4 -> 16, of which waited for: 4 -> 8; matrix products, arithmetic and copies ran while one was open for 11% -> 11% of each run, Pallas kernels for 0% -> 0%
where the time goes in v1:
time: 545 us; the launch traced here: 541 us
  waiting for transfers between devices  328 us (60%)
  local copies, waits for them, and re-layouts  78.3 us (14%)
  matrix products  67.6 us (12%)
  starting transfers between devices  36.6 us (7%)
  between operations  16 us (3%)
  other arithmetic  14.2 us (3%)
    reduce_scatter x1, waiting for transfers between devices, local(): lax.psum_scatter(device_grad, 'fsdp', scatter_dimension=1, tiled=True)  123 us
    all_gather x1, waiting for transfers between devices, local(): lax.all_gather(jnp.transpose(down_weight, (1, 0, 2)), 'fsdp', axis=1, til...  108 us
    ppermute x7, waiting for transfers between devices, gather_dp(): lax.ppermute(piece, axis_name, ring_pairs(n, k))  54 us
    ppermute x7, waiting for transfers between devices, scatter_sum_dp(): lax.ppermute(piece, axis_name, ring_pairs(n, k)).astype(jnp.float32)  42.9 us
    unnamed x44, local copies, waits for them, and re-layouts  37.5 us
    dot_general x2, matrix products, local(): jnp.einsum('th,dh->td', hid_e, panel[e], preferred_element_type=jnp.float32)  29.8 us
    ppermute x7, starting transfers between devices, gather_dp(): lax.ppermute(piece, axis_name, ring_pairs(n, k))  24.8 us
    dot_general x2, matrix products, local(): jnp.dot(slot_cot[a:b], panel[e], preferred_element_type=jnp.float32)  17.7 us
  transfers between devices with their start and end apart: 16, of which 8 were waited for; matrix products, arithmetic and copies ran while one was open for 11% of the time, Pallas kernels for 0%

profile of v1, /device:TPU:1, one launch (start us, length us, event | category | flops | bytes accessed | tf_op | source)
XLA Modules:
  0.0 540.9 jit_solution(17330327143071226754)
XLA Ops:
  7.2 1.4 copy.21
  8.6 5.6 %collective-permute-start.7 = (bf16[768,512]{0,1:T(8,128)(2,1)S(1)}, bf16[768,512]{0,1:T(8,128)(2,1)S(1)}, u32[]{:S(2)}, u32[]{:S(2)}) collective-permute-start(bf16[768,512]{0,1:T(8,128)(2,1)S(1)} %copy.21), channel_id=1, source_target_pairs={{0,7},{1,0},{2,1},{3,2},{4,3},{5,4},{6,5},{7,6},{8,15},{9,8},{10,9... | collective-permute-start | bytes 2359304 | tf_op jit(solution)/shard_map/ppermute | solution.py:19
  14.3 3.1 collective-permute-start.10
  18.3 1.3 fusion.63
  21.0 2.0 broadcast_select_fusion.2
  23.9 7.6 %collective-permute-done.7 = bf16[768,512]{0,1:T(8,128)(2,1)S(1)} collective-permute-done((bf16[768,512]{0,1:T(8,128)(2,1)S(1)}, bf16[768,512]{0,1:T(8,128)(2,1)S(1)}, u32[]{:S(2)}, u32[]{:S(2)}) %collective-permute-start.7) | collective-permute-done | bytes 786464 | tf_op jit(solution)/shard_map/ppermute | solution.py:19
  32.5 33.6 %collective-permute-done.8 = bf16[768,512]{0,1:T(8,128)(2,1)S(1)} collective-permute-done((bf16[768,512]{0,1:T(8,128)(2,1)S(1)}, bf16[768,512]{0,1:T(8,128)(2,1)S(1)}, u32[]{:S(2)}, u32[]{:S(2)}) %collective-permute-start.8) | collective-permute-done | bytes 786464 | tf_op jit(solution)/shard_map/ppermute | solution.py:19
  66.1 15.9 %collective-permute-start.13 = (bf16[768,512]{0,1:T(8,128)(2,1)S(1)}, bf16[768,512]{0,1:T(8,128)(2,1)S(1)}, u32[]{:S(2)}, u32[]{:S(2)}) collective-permute-start(bf16[768,512]{0,1:T(8,128)(2,1)S(1)} %copy.21), channel_id=1, source_target_pairs={{0,1},{1,2},{2,3},{3,4},{4,5},{5,6},{6,7},{7,0},{8,9},{9,10},{10,1... | collective-permute-start | bytes 2359304 | tf_op jit(solution)/shard_map/ppermute | solution.py:19
  83.9 2.1 bitcast_dynamic-update-slice_fusion.6
  86.0 2.1 bitcast_dynamic-update-slice_fusion.4
  89.0 12.8 %collective-permute-done.13 = bf16[768,512]{0,1:T(8,128)(2,1)S(1)} collective-permute-done((bf16[768,512]{0,1:T(8,128)(2,1)S(1)}, bf16[768,512]{0,1:T(8,128)(2,1)S(1)}, u32[]{:S(2)}, u32[]{:S(2)}) %collective-permute-start.13) | collective-permute-done | bytes 786464 | tf_op jit(solution)/shard_map/ppermute | solution.py:19
  106.7 2.1 bitcast_dynamic-update-slice_fusion.7
  108.8 2.1 bitcast_dynamic-update-slice_fusion.5
  112.7 3.2 constant_dynamic-slice_fusion
  115.9 5.4 multiply_convert_fusion
  121.3 7.4 %convert_bitcast_fusion = bf16[1,4096,1024]{2,1,0:T(8,128)(2,1)S(1)} fusion(pred[640]{0:T(1024)(128)(4,1)S(1)} %broadcast_bitcast_fusion, bf16[768,4096]{1,0:T(8,128)(2,1)S(1)} %multiply_convert_fusion, bf16[768,1024]{1,0:T(8,128)(2,1)S(1)} %copy-done.5), kind=kOutput, calls=%fused_computation.11 | convolution fusion | flops 5375524864 | bytes 14943232 | tf_op jit(solution)/shard_map/sd,sh->dh/dot_general | solution.py:69
  128.7 7.4 %convert_bitcast_fusion.1 = bf16[1,4096,1024]{2,1,0:T(8,128)(2,1)S(1)} fusion(pred[640]{0:T(1024)(128)(4,1)S(1)} %broadcast_bitcast_fusion.1, bf16[768,4096]{1,0:T(8,128)(2,1)S(1)} %multiply_convert_fusion, bf16[768,1024]{1,0:T(8,128)(2,1)S(1)} %copy-done.5), kind=kOutput, calls=%fused_computation.12 | convolution fusion | flops 5375524864 | bytes 14943232 | tf_op jit(solution)/shard_map/sd,sh->dh/dot_general | solution.py:69
  136.1 6.8 %pad_maximum_fusion = bf16[2,4096,1024]{2,1,0:T(8,128)(2,1)} fusion(bf16[1,4096,1024]{2,1,0:T(8,128)(2,1)S(1)} %convert_bitcast_fusion, bf16[1,4096,1024]{2,1,0:T(8,128)(2,1)S(1)} %convert_bitcast_fusion.1), kind=kLoop, calls=%fused_computation.6 | loop fusion | flops 8388608 | bytes 33554432 | tf_op jit(solution)/shard_map/stack | solution.py:73
  144.1 1.2 copy.50
  145.5 3.6 scatter_custom_fusion.1
  149.2 3.4 scatter_custom_fusion
  152.6 3.4 scatter_custom_fusion.2
  156.0 3.8 scatter_custom_fusion.3
  159.9 3.2 gather_fusion.1
  163.1 3.2 gather_fusion
  166.4 123.5 %reduce-scatter.2.cloned.1.call-done = bf16[2,256,1024]{2,1,0:T(8,128)(2,1)} async-done(((bf16[2,4096,1024]{2,1,0:T(8,128)(2,1)}), bf16[2,256,1024]{2,1,0:T(8,128)(2,1)}) %reduce-scatter.2.cloned.1.call-update) | async-done | bytes 1048592 | tf_op jit(solution)/shard_map/reduce_scatter | solution.py:74
  289.9 1.4 fusion.40
  291.3 2.0 copy.29
  293.4 107.7 %all-gather.2.cloned.1.call-done = bf16[2,4096,1024]{2,1,0:T(8,128)(2,1)} async-done(((bf16[2,256,1024]{2,1,0:T(8,128)(2,1)}), bf16[2,4096,1024]{2,1,0:T(8,128)(2,1)}) %all-gather.2.cloned.1.call-update) | async-done | bytes 16777232 | tf_op jit(solution)/shard_map/all_gather | solution.py:52
  401.1 14.3 %fusion.1 = f32[768,4096]{1,0:T(8,128)} fusion(bf16[2,4096,1024]{2,1,0:T(8,128)(2,1)} %all-gather.2.cloned.1.call-done, bf16[768,1024]{1,0:T(8,128)(2,1)S(1)} %copy-done.5, s32[768]{0:T(1024)S(1)} %scatter_custom_fusion.1, pred[768]{0:T(1024)(128)(4,1)S(1)} %scatter_custom_fusion), kind=kOutput, calls=%fused_computation.14 | convolution fusion | flops 7652376576 | bytes 22548224 | tf_op jit(solution)/shard_map/th,dh->td/dot_general | solution.py:89
  415.4 15.5 %add_convert_fusion = bf16[768,4096]{1,0:T(8,128)(2,1)} fusion(f32[768,4096]{1,0:T(8,128)} %fusion.1, bf16[2,4096,1024]{2,1,0:T(8,128)(2,1)} %all-gather.2.cloned.1.call-done, f32[768]{0:T(1024)S(1)} %broadcast_select_fusion, f32[768]{0:T(1024)S(1)} %broadcast_select_fusion.1, bf16[768,1024]{1,0:T(8,128)(2,1)S(1)} %copy-done.5, ...), kind=kOutput, calls=%fused_computation.8 | convolution fusion | flops 7664959488 | bytes 28845824 | tf_op jit(solution)/shard_map/th,dh->td/dot_general | solution.py:89
  430.9 7.0 %copy.38 = bf16[96,8,8,512]{3,2,1,0:T(8,128)(2,1)S(1)} copy(bf16[96,8,8,512]{3,1,2,0:T(8,128)(2,1)} %bitcast.91) | data formatting | bytes 12582912
  437.8 14.4 %constant_dynamic-slice_fusion.8 = (bf16[768,1,512]{2,1,0:T(2,128)(2,1)}, bf16[768,1,512]{2,1,0:T(2,128)(2,1)S(1)}, bf16[768,1,512]{2,1,0:T(2,128)(2,1)}, bf16[7...) fusion(bf16[768,8,512]{2,1,0:T(8,128)(2,1)S(1)} %bitcast.90, ...), kind=kLoop, calls=%fused_computation.111 | loop fusion | bytes 12582944 | tf_op jit(solution)/shard_map/jit(dynamic_index_in_dim)/dynamic_slice | solution.py:28
  452.2 1.8 copy.57
  454.4 1.6 copy.56
  456.0 1.3 collective-permute-start.1
  457.3 1.6 copy.55
  458.9 2.9 collective-permute-start.2
  462.1 1.7 collective-permute-start.3
  464.0 2.0 collective-permute-start.4
  466.0 9.7 %fusion = bf16[640,1024]{1,0:T(8,128)(2,1)S(1)} fusion(bf16[2,4096,1024]{2,1,0:T(8,128)(2,1)} %all-gather.2.cloned.1.call-done, bf16[768,4096]{1,0:T(8,128)(2,1)} %copy-done.6), kind=kOutput, calls=%fused_computation.13 | convolution fusion | flops 5368709120 | bytes 14942208 | tf_op jit(solution)/shard_map/dot_general | solution.py:98
  477.4 32.0 %collective-permute-done.1 = bf16[768,512]{1,0:T(8,128)(2,1)S(1)} collective-permute-done((bf16[768,512]{1,0:T(8,128)(2,1)S(1)}, bf16[768,512]{1,0:T(8,128)(2,1)S(1)}, u32[]{:S(2)}, u32[]{:S(2)}) %collective-permute-start.1) | collective-permute-done | bytes 786464 | tf_op jit(solution)/shard_map/ppermute | solution.py:31
  509.3 2.3 collective-permute-start.6
  511.6 7.9 %fusion.2 = bf16[640,1024]{1,0:T(8,128)(2,1)S(1)} fusion(bf16[2,4096,1024]{2,1,0:T(8,128)(2,1)} %all-gather.2.cloned.1.call-done, bf16[768,4096]{1,0:T(8,128)(2,1)S(1)} %bitcast.103), kind=kOutput, calls=%fused_computation.15 | convolution fusion | flops 5368709120 | bytes 14942208 | tf_op jit(solution)/shard_map/dot_general | solution.py:98
  519.8 1.3 pad_maximum_fusion.1
  521.1 6.3 %collective-permute-done.3 = bf16[768,512]{1,0:T(8,128)(2,1)S(1)} collective-permute-done((bf16[768,512]{1,0:T(8,128)(2,1)S(1)}, bf16[768,512]{1,0:T(8,128)(2,1)S(1)}, u32[]{:S(2)}, u32[]{:S(2)}) %collective-permute-start.3) | collective-permute-done | bytes 786464 | tf_op jit(solution)/shard_map/ppermute | solution.py:31
  527.4 4.6 collective-permute-done.5
  532.0 1.8 fusion.32
  (71 shorter events, 16.6 us)
Async XLA Ops:
  7.2 282.7 %reduce-scatter.2.cloned.1.call-start = ((), (), s32[]{:S(2)}) async-start(), calls=%async_computation.2 | async-start | bytes 17825792 | tf_op jit(solution)/shard_map/reduce_scatter | solution.py:74
  8.6 22.8 %collective-permute-start.7 = (bf16[768,512]{0,1:T(8,128)(2,1)S(1)}, bf16[768,512]{0,1:T(8,128)(2,1)S(1)}, u32[]{:S(2)}, u32[]{:S(2)}) collective-permute-start(bf16[768,512]{0,1:T(8,128)(2,1)S(1)} %copy.21), channel_id=1, source_target_pairs={{0,7},{1,0},{2,1},{3,2},{4,3},{5,4},{6,5},{7,6},{8,15},{9,8},{10,9... | collective-permute-start | bytes 2359304 | tf_op jit(solution)/shard_map/ppermute | solution.py:19
  14.2 51.9 %collective-permute-start.8 = (bf16[768,512]{0,1:T(8,128)(2,1)S(1)}, bf16[768,512]{0,1:T(8,128)(2,1)S(1)}, u32[]{:S(2)}, u32[]{:S(2)}) collective-permute-start(bf16[768,512]{0,1:T(8,128)(2,1)S(1)} %copy.21), channel_id=1, source_target_pairs={{0,6},{1,7},{2,0},{3,1},{4,2},{5,3},{6,4},{7,5},{8,14},{9,15},{10,... | collective-permute-start | bytes 2359304 | tf_op jit(solution)/shard_map/ppermute | solution.py:19
  14.3 68.7 %collective-permute-start.9 = (bf16[768,512]{0,1:T(8,128)(2,1)S(1)}, bf16[768,512]{0,1:T(8,128)(2,1)S(1)}, u32[]{:S(2)}, u32[]{:S(2)}) collective-permute-start(bf16[768,512]{0,1:T(8,128)(2,1)S(1)} %copy.21), channel_id=1, source_target_pairs={{0,5},{1,6},{2,7},{3,0},{4,1},{5,2},{6,3},{7,4},{8,13},{9,14},{10,... | collective-permute-start | bytes 2359304 | tf_op jit(solution)/shard_map/ppermute | solution.py:19
  14.3 69.6 %collective-permute-start.10 = (bf16[768,512]{0,1:T(8,128)(2,1)S(1)}, bf16[768,512]{0,1:T(8,128)(2,1)}, u32[]{:S(2)}, u32[]{:S(2)}) collective-permute-start(bf16[768,512]{0,1:T(8,128)(2,1)S(1)} %copy.21), channel_id=1, source_target_pairs={{0,4},{1,5},{2,6},{3,7},{4,0},{5,1},{6,2},{7,3},{8,12},{9,13},{10,... | collective-permute-start | bytes 2359304 | tf_op jit(solution)/shard_map/ppermute | solution.py:19
  17.4 68.6 %collective-permute-start.11 = (bf16[768,512]{0,1:T(8,128)(2,1)S(1)}, bf16[768,512]{0,1:T(8,128)(2,1)}, u32[]{:S(2)}, u32[]{:S(2)}) collective-permute-start(bf16[768,512]{0,1:T(8,128)(2,1)S(1)} %copy.21), channel_id=1, source_target_pairs={{0,3},{1,4},{2,5},{3,6},{4,7},{5,0},{6,1},{7,2},{8,11},{9,12},{10,... | collective-permute-start | bytes 2359304 | tf_op jit(solution)/shard_map/ppermute | solution.py:19
  31.5 56.6 %collective-permute-start.12 = (bf16[768,512]{0,1:T(8,128)(2,1)S(1)}, bf16[768,512]{0,1:T(8,128)(2,1)S(1)}, u32[]{:S(2)}, u32[]{:S(2)}) collective-permute-start(bf16[768,512]{0,1:T(8,128)(2,1)S(1)} %copy.21), channel_id=1, source_target_pairs={{0,2},{1,3},{2,4},{3,5},{4,6},{5,7},{6,0},{7,1},{8,10},{9,11},{10,... | collective-permute-start | bytes 2359304 | tf_op jit(solution)/shard_map/ppermute | solution.py:19
  66.1 35.7 %collective-permute-start.13 = (bf16[768,512]{0,1:T(8,128)(2,1)S(1)}, bf16[768,512]{0,1:T(8,128)(2,1)S(1)}, u32[]{:S(2)}, u32[]{:S(2)}) collective-permute-start(bf16[768,512]{0,1:T(8,128)(2,1)S(1)} %copy.21), channel_id=1, source_target_pairs={{0,1},{1,2},{2,3},{3,4},{4,5},{5,6},{6,7},{7,0},{8,9},{9,10},{10,1... | collective-permute-start | bytes 2359304 | tf_op jit(solution)/shard_map/ppermute | solution.py:19
  112.7 3.2 copy-start.4
  115.9 5.4 copy-start.5
  121.3 7.4 %copy-start.6 = (bf16[768,4096]{1,0:T(8,128)(2,1)}, bf16[768,4096]{1,0:T(8,128)(2,1)S(1)}, u32[]{:S(2)}) copy-start(bf16[768,4096]{1,0:T(8,128)(2,1)S(1)} %multiply_convert_fusion) | copy-start | bytes 18874372
  142.9 1.2 copy-start.3
  142.9 258.2 %all-gather.2.cloned.1.call-start = ((), (), s32[]{:S(2)}) async-start(), calls=%async_computation.1 | async-start | bytes 17825792 | tf_op jit(solution)/shard_map/all_gather | solution.py:52
  452.2 9.6 %copy-start.1 = (bf16[768,1,512]{2,1,0:T(2,128)(2,1)S(1)}, bf16[768,1,512]{2,1,0:T(2,128)(2,1)}, u32[]{:S(2)}) copy-start(bf16[768,1,512]{2,1,0:T(2,128)(2,1)} %get-tuple-element.14) | copy-start | bytes 2359300
  452.2 11.5 %copy-start = (bf16[768,1,512]{2,1,0:T(2,128)(2,1)S(1)}, bf16[768,1,512]{2,1,0:T(2,128)(2,1)}, u32[]{:S(2)}) copy-start(bf16[768,1,512]{2,1,0:T(2,128)(2,1)} %get-tuple-element.13) | copy-start | bytes 2359300
  454.0 22.2 %collective-permute-start = (bf16[768,512]{1,0:T(8,128)(2,1)S(1)}, bf16[768,512]{1,0:T(8,128)(2,1)S(1)}, u32[]{:S(2)}, u32[]{:S(2)}) collective-permute-start(bf16[768,512]{1,0:T(8,128)(2,1)S(1)} %bitcast.100), channel_id=1, source_target_pairs={{0,1},{1,2},{2,3},{3,4},{4,5},{5,6},{6,7},{7,0},{8,9},{9,10},{10,1... | collective-permute-start | bytes 2359304 | tf_op jit(solution)/shard_map/ppermute | solution.py:31
  456.0 53.4 %collective-permute-start.1 = (bf16[768,512]{1,0:T(8,128)(2,1)S(1)}, bf16[768,512]{1,0:T(8,128)(2,1)S(1)}, u32[]{:S(2)}, u32[]{:S(2)}) collective-permute-start(bf16[768,512]{1,0:T(8,128)(2,1)S(1)} %bitcast.99), channel_id=1, source_target_pairs={{0,2},{1,3},{2,4},{3,5},{4,6},{5,7},{6,0},{7,1},{8,10},{9,11},{10,... | collective-permute-start | bytes 2359304 | tf_op jit(solution)/shard_map/ppermute | solution.py:31
  458.9 62.1 %collective-permute-start.2 = (bf16[768,512]{1,0:T(8,128)(2,1)S(1)}, bf16[768,512]{1,0:T(8,128)(2,1)S(1)}, u32[]{:S(2)}, u32[]{:S(2)}) collective-permute-start(bf16[768,512]{1,0:T(8,128)(2,1)S(1)} %bitcast.94), channel_id=1, source_target_pairs={{0,3},{1,4},{2,5},{3,6},{4,7},{5,0},{6,1},{7,2},{8,11},{9,12},{10,... | collective-permute-start | bytes 2359304 | tf_op jit(solution)/shard_map/ppermute | solution.py:31
  462.1 65.3 %collective-permute-start.3 = (bf16[768,512]{1,0:T(8,128)(2,1)S(1)}, bf16[768,512]{1,0:T(8,128)(2,1)S(1)}, u32[]{:S(2)}, u32[]{:S(2)}) collective-permute-start(bf16[768,512]{1,0:T(8,128)(2,1)S(1)} %bitcast.95), channel_id=1, source_target_pairs={{0,4},{1,5},{2,6},{3,7},{4,0},{5,1},{6,2},{7,3},{8,12},{9,13},{10,... | collective-permute-start | bytes 2359304 | tf_op jit(solution)/shard_map/ppermute | solution.py:31
  464.0 47.6 %slice-start = ((s8[6291456]{0:T(1024)(128)(4,1)}), s8[4194304]{0:T(1024)(128)(4,1)S(1)}, s32[]{:S(2)}) async-start(s8[6291456]{0:T(1024)(128)(4,1)} %bitcast.102), calls=%async_computation.3 | async-start | bytes 8388608
  464.0 47.6 %slice-start.1 = ((s8[6291456]{0:T(1024)(128)(4,1)}), s8[2097152]{0:T(1024)(128)(4,1)S(1)}, s32[]{:S(2)}) async-start(s8[6291456]{0:T(1024)(128)(4,1)} %bitcast.102), calls=%async_computation.4 | async-start | bytes 4194304
  464.0 63.4 %collective-permute-start.4 = (bf16[768,512]{1,0:T(8,128)(2,1)S(1)}, bf16[768,512]{1,0:T(8,128)(2,1)S(1)}, u32[]{:S(2)}, u32[]{:S(2)}) collective-permute-start(bf16[768,512]{1,0:T(8,128)(2,1)S(1)} %bitcast.96), channel_id=1, source_target_pairs={{0,5},{1,6},{2,7},{3,0},{4,1},{5,2},{6,3},{7,4},{8,13},{9,14},{10,... | collective-permute-start | bytes 2359304 | tf_op jit(solution)/shard_map/ppermute | solution.py:31
  476.2 55.8 %collective-permute-start.5 = (bf16[768,512]{1,0:T(8,128)(2,1)S(1)}, bf16[768,512]{1,0:T(8,128)(2,1)S(1)}, u32[]{:S(2)}, u32[]{:S(2)}) collective-permute-start(bf16[768,512]{1,0:T(8,128)(2,1)S(1)} %bitcast.98), channel_id=1, source_target_pairs={{0,6},{1,7},{2,0},{3,1},{4,2},{5,3},{6,4},{7,5},{8,14},{9,15},{10,... | collective-permute-start | bytes 2359304 | tf_op jit(solution)/shard_map/ppermute | solution.py:31
  509.3 22.6 %collective-permute-start.6 = (bf16[768,512]{1,0:T(8,128)(2,1)S(1)}, bf16[768,512]{1,0:T(8,128)(2,1)S(1)}, u32[]{:S(2)}, u32[]{:S(2)}) collective-permute-start(bf16[768,512]{1,0:T(8,128)(2,1)S(1)} %bitcast.97), channel_id=1, source_target_pairs={{0,7},{1,0},{2,1},{3,2},{4,3},{5,4},{6,5},{7,6},{8,15},{9,8},{10,9... | collective-permute-start | bytes 2359304 | tf_op jit(solution)/shard_map/ppermute | solution.py:31
  519.6 12.4 %copy-start.2 = (bf16[768,1,512]{2,1,0:T(2,128)(2,1)S(1)}, bf16[768,1,512]{2,1,0:T(2,128)(2,1)}, u32[]{:S(2)}) copy-start(bf16[768,1,512]{2,1,0:T(2,128)(2,1)} %get-tuple-element.11) | copy-start | bytes 2359300
Sparse Core Ops, SparseCore 0:
  143.0 146.8 reduce-scatter.1
  293.0 108.0 all-gather.1

commit v2 on v1

--- a/solution.py
+++ b/solution.py
@@ -13,21 +13,20 @@
     return [(i, (i + k) % n) for i in range(n)]
 
 
-def gather_dp(piece, axis_name):
+def gather_major(piece, axis_name):
     n = lax.axis_size(axis_name)
     me = lax.axis_index(axis_name)
     recv = [piece] + [lax.ppermute(piece, axis_name, ring_pairs(n, k)) for k in range(1, n)]
-    arr = jnp.stack([recv[(-m) % n] for m in range(n)], axis=1)
-    arr2 = jnp.concatenate([arr, arr], axis=1)
-    return lax.dynamic_slice_in_dim(arr2, (n - me) % n, n, axis=1)
+    arr = jnp.stack([recv[(-m) % n] for m in range(n)] * 2, axis=0)
+    return lax.dynamic_slice_in_dim(arr, (n - me) % n, n, axis=0)
 
 
-def scatter_sum_dp(full, axis_name):
+def scatter_sum_major(full, axis_name):
     n = lax.axis_size(axis_name)
     me = lax.axis_index(axis_name)
-    total = lax.dynamic_index_in_dim(full, me, axis=1, keepdims=False).astype(jnp.float32)
+    total = lax.dynamic_index_in_dim(full, me, axis=0, keepdims=False).astype(jnp.float32)
     for k in range(1, n):
-        piece = lax.dynamic_index_in_dim(full, (me + k) % n, axis=1, keepdims=False)
+        piece = lax.dynamic_index_in_dim(full, (me + k) % n, axis=0, keepdims=False)
         total = total + lax.ppermute(piece, axis_name, ring_pairs(n, k)).astype(jnp.float32)
     return total.astype(jnp.bfloat16)
 
@@ -36,6 +35,7 @@
     slot_count, hidden_width = hidden.shape
     block_count = block_expert.shape[0]
     n_dp = lax.axis_size("dp")
+    part_width = cotangent.shape[1]
     positions = jnp.arange(slot_count, dtype=jnp.int32)
     blocks = positions // BLK
     live_rows = expert_rows[0]
@@ -51,26 +51,30 @@
 
     panel = lax.all_gather(jnp.transpose(down_weight, (1, 0, 2)), "fsdp", axis=1, tiled=True)
     model_width = panel.shape[1]
+    panel_parts = panel.reshape(EXPERTS, n_dp, part_width, hidden_width)
 
-    full_cot = gather_dp(cotangent, "dp").reshape(slot_count, model_width)
+    full_cot = gather_major(cotangent, "dp")
     tok_hot = (slot_token[:, None] == positions[None, :]).astype(jnp.bfloat16)
-    picked = jnp.dot(tok_hot, full_cot, preferred_element_type=jnp.float32)
-    slot_cot = (slot_scale[:, None] * picked).astype(jnp.bfloat16)
+    picked = jnp.einsum("st,jtc->jsc", tok_hot, full_cot, preferred_element_type=jnp.float32)
+    slot_cot = (slot_scale[None, :, None] * picked).astype(jnp.bfloat16)
 
     lo = (block_count - 1) * BLK
     masks = [slot_expert == e for e in range(EXPERTS)]
     windows = [(0, lo), (BLK, slot_count)]
 
+    cot_flat = jnp.transpose(slot_cot, (1, 0, 2)).reshape(slot_count, model_width)
     grads = []
     for e in range(EXPERTS):
         a, b = windows[e]
-        cot_e = jnp.where(masks[e][a:b, None], slot_cot[a:b], jnp.zeros_like(slot_cot[a:b]))
+        cot_w = cot_flat[a:b]
+        cot_e = jnp.where(masks[e][a:b, None], cot_w, jnp.zeros_like(cot_w))
         grads.append(
             jnp.einsum("sd,sh->dh", cot_e, hidden[a:b], preferred_element_type=jnp.float32).astype(
                 jnp.bfloat16
             )
         )
     device_grad = jnp.stack(grads, axis=0)
+    device_grad, panel_parts = lax.optimization_barrier((device_grad, panel_parts))
     summed = lax.psum_scatter(device_grad, "fsdp", scatter_dimension=1, tiled=True).astype(
         jnp.float32
     )
@@ -86,16 +90,19 @@
         scale_e = jnp.where(has, slot_scale[inv], 0.0)
         sel = ((inv[:, None] == positions[None, :]) & has[:, None]).astype(jnp.bfloat16)
         hid_e = jnp.dot(sel, hidden, preferred_element_type=jnp.float32).astype(jnp.bfloat16)
-        out_e = jnp.einsum("th,dh->td", hid_e, panel[e], preferred_element_type=jnp.float32)
-        term = scale_e[:, None] * out_e
+        out_e = jnp.einsum("th,jch->jtc", hid_e, panel_parts[e], preferred_element_type=jnp.float32)
+        term = scale_e[None, :, None] * out_e
         combined = term if combined is None else combined + term
-    token_part = combined.astype(jnp.bfloat16).reshape(slot_count, n_dp, model_width // n_dp)
-    expert_out = scatter_sum_dp(token_part, "dp")
+    expert_out = scatter_sum_major(combined.astype(jnp.bfloat16), "dp")
 
     gh = []
     for e in range(EXPERTS):
         a, b = windows[e]
-        gh.append(jnp.dot(slot_cot[a:b], panel[e], preferred_element_type=jnp.float32))
+        gh.append(
+            jnp.einsum(
+                "jsc,jch->sh", slot_cot[:, a:b], panel_parts[e], preferred_element_type=jnp.float32
+            )
+        )
     head = gh[0][:BLK]
     mid = jnp.where(masks[0][BLK:lo, None], gh[0][BLK:lo], gh[1][: lo - BLK])
     tail = gh[1][lo - BLK :]

time: 545 us -> 395 us (0.72)
  waiting for transfers between devices: 328 us -> 126 us
  starting transfers between devices: 36.6 us -> 91.3 us
  local copies, waits for them, and re-layouts: 78.3 us -> 63.4 us
  other arithmetic: 14.2 us -> 25.2 us
    all_gather x1, waiting for transfers between devices: 108 us -> 0.01 us  [local(): lax.all_gather(jnp.transpose(down_weight, (1, 0, 2)), 'fsdp', axis=1, til...]
    reduce_scatter x1, waiting for transfers between devices: 123 us -> 26.3 us  [local(): lax.psum_scatter(device_grad, 'fsdp', scatter_dimension=1, tiled=True)]
    ppermute x14, starting transfers between devices: 36.5 us -> 91.2 us  [the longest x7 53.8 us: gather_major(): lax.ppermute(piece, axis_name, ring_pairs(n, k))]
    unnamed x44 -> x42, local copies, waits for them, and re-layouts: 37.5 us -> 12.6 us
    dynamic_slice x2 -> x0, local copies, waits for them, and re-layouts: 17.6 us -> none  [the longest x1 14.4 us: scatter_sum_dp(): lax.dynamic_index_in_dim(full, me, axis=1, keepdims=False)]
    all_gather x0 -> x1, local copies, waits for them, and re-layouts: none -> 16.4 us  [local(): lax.all_gather(jnp.transpose(down_weight, (1, 0, 2)), 'fsdp', axis=1, til...]
    slice x3 -> x4, local copies, waits for them, and re-layouts: 0.23 us -> 9.82 us  [the longest x1 9.6 us: local(): cot_w = cot_flat[a:b]]
    select_n x0 -> x1, other arithmetic: none -> 8.92 us  [local(): cot_e = jnp.where(masks[e][a:b, None], cot_w, jnp.zeros_like(cot_w))]
  transfers between devices with their start and end apart: 16 -> 16, of which waited for: 8 -> 7; matrix products, arithmetic and copies ran while one was open for 11% -> 35% of each run, Pallas kernels for 0% -> 0%
where the time goes in v2:
time: 395 us; the launch traced here: 391 us
  waiting for transfers between devices  126 us (32%)
  starting transfers between devices  91.3 us (23%)
  matrix products  69.3 us (18%)
  local copies, waits for them, and re-layouts  63.4 us (16%)
  other arithmetic  25.2 us (6%)
  between operations  16 us (4%)
    ppermute x7, starting transfers between devices, gather_major(): lax.ppermute(piece, axis_name, ring_pairs(n, k))  53.8 us
    ppermute x7, waiting for transfers between devices, scatter_sum_major(): lax.ppermute(piece, axis_name, ring_pairs(n, k)).astype(jnp.float32)  49.7 us
    ppermute x7, waiting for transfers between devices, gather_major(): lax.ppermute(piece, axis_name, ring_pairs(n, k))  48.8 us
    ppermute x7, starting transfers between devices, scatter_sum_major(): lax.ppermute(piece, axis_name, ring_pairs(n, k)).astype(jnp.float32)  37.4 us
    dot_general x2, matrix products, local(): jnp.einsum('th,jch->jtc', hid_e, panel_parts[e], preferred_element_type=j...  28.1 us
    reduce_scatter x1, waiting for transfers between devices, local(): lax.psum_scatter(device_grad, 'fsdp', scatter_dimension=1, tiled=True)  26.3 us
    dot_general x2, matrix products, local(): jnp.einsum('sd,sh->dh', cot_e, hidden[a:b], preferred_element_type=jnp.fl...  16.9 us
    all_gather x1, local copies, waits for them, and re-layouts, local(): lax.all_gather(jnp.transpose(down_weight, (1, 0, 2)), 'fsdp', axis=1, til...  16.4 us
  transfers between devices with their start and end apart: 16, of which 7 were waited for; matrix products, arithmetic and copies ran while one was open for 35% of the time, Pallas kernels for 0%

profile of v2, /device:TPU:1, one launch (start us, length us, event | category | flops | bytes accessed | tf_op | source)
XLA Modules:
  0.0 390.7 jit_solution(15861052641669957839)
XLA Ops:
  7.2 0.7 all-gather.2.cloned.1.call-update
  7.9 1.4 copy.36
  9.4 5.6 %collective-permute-start = (bf16[768,512]{0,1:T(8,128)(2,1)S(1)}, bf16[768,512]{0,1:T(8,128)(2,1)S(1)}, u32[]{:S(2)}, u32[]{:S(2)}) collective-permute-start(bf16[768,512]{0,1:T(8,128)(2,1)S(1)} %copy.36), channel_id=1, source_target_pairs={{0,7},{1,0},{2,1},{3,2},{4,3},{5,4},{6,5},{7,6},{8,15},{9,8},{10,9... | collective-permute-start | bytes 2359304 | tf_op jit(solution)/shard_map/ppermute | solution.py:19
  15.1 3.1 collective-permute-start.3
  18.2 1.3 fusion.84
  21.5 2.1 compare_select_fusion.3
  23.8 0.7 broadcast_select_fusion.2
  24.5 13.0 %collective-permute-done = bf16[768,512]{0,1:T(8,128)(2,1)S(1)} collective-permute-done((bf16[768,512]{0,1:T(8,128)(2,1)S(1)}, bf16[768,512]{0,1:T(8,128)(2,1)S(1)}, u32[]{:S(2)}, u32[]{:S(2)}) %collective-permute-start) | collective-permute-done | bytes 786464 | tf_op jit(solution)/shard_map/ppermute | solution.py:19
  37.6 45.0 %collective-permute-start.6 = (bf16[768,512]{0,1:T(8,128)(2,1)S(1)}, bf16[768,512]{0,1:T(8,128)(2,1)S(1)}, u32[]{:S(2)}, u32[]{:S(2)}) collective-permute-start(bf16[768,512]{0,1:T(8,128)(2,1)S(1)} %copy.36), channel_id=1, source_target_pairs={{0,1},{1,2},{2,3},{3,4},{4,5},{5,6},{6,7},{7,0},{8,9},{9,10},{10,1... | collective-permute-start | bytes 2359304 | tf_op jit(solution)/shard_map/ppermute | solution.py:19
  82.7 1.2 bitcast_dynamic-update-slice_fusion.6
  83.9 3.4 collective-permute-done.4
  87.3 1.2 bitcast_dynamic-update-slice_fusion.4
  88.6 32.4 %collective-permute-done.6 = bf16[768,512]{0,1:T(8,128)(2,1)S(1)} collective-permute-done((bf16[768,512]{0,1:T(8,128)(2,1)S(1)}, bf16[768,512]{0,1:T(8,128)(2,1)S(1)}, u32[]{:S(2)}, u32[]{:S(2)}) %collective-permute-start.6) | collective-permute-done | bytes 786464 | tf_op jit(solution)/shard_map/ppermute | solution.py:19
  121.3 1.2 bitcast_dynamic-update-slice_fusion.7
  122.5 1.2 bitcast_dynamic-update-slice_fusion.5
  123.8 7.4 %multiply_convert_fusion = bf16[8,512,768]{2,1,0:T(8,128)(2,1)} fusion(f32[768]{0:T(1024)S(1)} %broadcast_select_fusion.2, bf16[16,768,512]{1,2,0:T(8,128)(2,1)S(1)} %bitcast_dynamic-update-slice_fusion.1, s32[]{:T(128)S(6)} %select_n.129, s32[768]{0:T(1024)S(1)} %copy-done.4), kind=kOutput, calls=%fused_computation.8 | convolution fusion | flops 4838719488 | bytes 12591108 | tf_op jit(solution)/shard_map/st,jtc->jsc/dot_general | solution.py:58
  131.3 9.6 %fusion.83 = (bf16[640,8,512]{0,2,1:T(8,128)(2,1)}, bf16[640,8,512]{0,2,1:T(8,128)(2,1)}) fusion(bf16[768,8,512]{0,2,1:T(8,128)(2,1)} %bitcast.134), kind=kLoop, calls=%fused_computation.126 | loop fusion | bytes 20971520 | tf_op jit(solution)/shard_map/slice | solution.py:69
  140.9 8.9 %bitcast_select_fusion = (bf16[640,4096]{0,1:T(8,128)(2,1)}, bf16[640,4096]{0,1:T(8,128)(2,1)}) fusion(bf16[640,8,512]{0,2,1:T(8,128)(2,1)} %get-tuple-element.26, pred[640]{0:T(1024)(128)(4,1)S(1)} %broadcast_bitcast_fusion, bf16[640,8,512]{0,2,1:T(8,128)(2,1)} %get-tuple-element.25, pred[640]{0:T(1024)(128)(4,1)S(1)} %broadcast_bitcast_fusion.1), kind=kLoop, calls=%fused_computation.27 | loop fusion | flops 5242880 | bytes 20972800 | tf_op jit(solution)/shard_map/jit(_where)/select_n | solution.py:70
  149.8 9.8 %convert_bitcast_fusion = bf16[1,4096,1024]{2,1,0:T(8,128)(2,1)S(1)} fusion(bf16[640,4096]{0,1:T(8,128)(2,1)} %get-tuple-element.33, bf16[768,1024]{1,0:T(8,128)(2,1)S(1)} %copy-done.5), kind=kOutput, calls=%fused_computation.17 | convolution fusion | flops 5372903424 | bytes 14942208 | tf_op jit(solution)/shard_map/sd,sh->dh/dot_general | solution.py:72
  159.6 7.1 %convert_bitcast_fusion.1 = bf16[1,4096,1024]{2,1,0:T(8,128)(2,1)S(1)} fusion(bf16[640,4096]{0,1:T(8,128)(2,1)S(1)} %copy-done.1, bf16[768,1024]{1,0:T(8,128)(2,1)S(1)} %copy-done.5), kind=kOutput, calls=%fused_computation.18 | convolution fusion | flops 5372903424 | bytes 14942208 | tf_op jit(solution)/shard_map/sd,sh->dh/dot_general | solution.py:72
  166.8 6.8 %pad_maximum_fusion = bf16[2,4096,1024]{2,1,0:T(8,128)(2,1)} fusion(bf16[1,4096,1024]{2,1,0:T(8,128)(2,1)S(1)} %convert_bitcast_fusion, bf16[1,4096,1024]{2,1,0:T(8,128)(2,1)S(1)} %convert_bitcast_fusion.1), kind=kLoop, calls=%fused_computation.6 | loop fusion | flops 8388608 | bytes 33554432 | tf_op jit(solution)/shard_map/stack | solution.py:76
  173.6 16.4 %copy.44 = bf16[2,4096,1024]{2,1,0:T(8,128)(2,1)} copy(bf16[2,4096,1024]{2,0,1:T(2,128)(2,1)} %all-gather.2.cloned.1.call-done) | data formatting | bytes 33554432 | tf_op jit(solution)/shard_map/all_gather | solution.py:52
  190.2 3.4 scatter_custom_fusion.3
  193.6 3.6 scatter_custom_fusion.2
  197.2 3.4 scatter_custom_fusion
  200.6 3.4 scatter_custom_fusion.1
  204.0 3.6 gather_fusion.1
  207.6 3.2 gather_fusion
  211.0 2.6 fusion.42
  213.6 16.0 %fusion.2 = f32[8,512,768]{2,1,0:T(8,128)} fusion(bf16[2,8,512,1024]{3,2,1,0:T(8,128)(2,1)} %bitcast.139, bf16[768,1024]{1,0:T(8,128)(2,1)} %param.7, s32[768]{0:T(1024)S(1)} %scatter_custom_fusion.3, pred[768]{0:T(1024)(128)(4,1)S(1)} %scatter_custom_fusion.2), kind=kOutput, calls=%fused_computation.11 | convolution fusion | flops 7652376576 | bytes 22548224 | tf_op jit(solution)/shard_map/th,jch->jtc/dot_general | solution.py:93
  229.6 12.1 %add_convert_fusion = bf16[8,512,768]{2,1,0:T(8,128)(2,1)S(1)} fusion(f32[8,512,768]{2,1,0:T(8,128)} %fusion.2, f32[768]{0:T(1024)S(1)} %broadcast_select_fusion, f32[768]{0:T(1024)S(1)} %broadcast_select_fusion.1, bf16[2,8,512,1024]{3,2,1,0:T(8,128)(2,1)} %bitcast.140, bf16[768,1024]{1,0:T(8,128)(2,1)} %fusion.42), kind=kOutput, calls=%fused_computation.7 | convolution fusion | flops 6455033856 | bytes 28841984 | tf_op jit(solution)/shard_map/th,jch->jtc/dot_general | solution.py:93
  241.6 2.6 copy-done
  244.2 2.5 dynamic-slice_bitcast_fusion.6
  246.7 4.9 %collective-permute-start.11 = (bf16[768,512]{0,1:T(8,128)(2,1)}, bf16[768,512]{0,1:T(8,128)(2,1)S(1)}, u32[]{:S(2)}, u32[]{:S(2)}) collective-permute-start(bf16[768,512]{0,1:T(8,128)(2,1)} %get-tuple-element.21), channel_id=1, source_target_pairs={{0,5},{1,6},{2,7},{3,0},{4,1},{5,2},{6,3},{7,4},{8,13},{9,14},{10,... | collective-permute-start | bytes 2359304 | tf_op jit(solution)/shard_map/ppermute | solution.py:30
  251.6 8.5 %fusion.29 = bf16[640,1024]{1,0:T(8,128)(2,1)S(1)} fusion(bf16[2,8,512,1024]{3,2,1,0:T(8,128)(2,1)} %bitcast.141, bf16[8,768,512]{1,2,0:T(8,128)(2,1)S(1)} %bitcast.137), kind=kOutput, calls=%fused_computation.40 | convolution fusion | flops 5368709120 | bytes 14942208 | tf_op jit(solution)/shard_map/jsc,jch->sh/dot_general | solution.py:102
  260.3 1.4 collective-permute-start.7
  261.7 0.8 collective-permute-done.10
  262.5 12.8 %collective-permute-start.8 = (bf16[768,512]{0,1:T(8,128)(2,1)S(1)}, bf16[768,512]{0,1:T(8,128)(2,1)}, u32[]{:S(2)}, u32[]{:S(2)}) collective-permute-start(bf16[768,512]{0,1:T(8,128)(2,1)S(1)} %copy-done.2), channel_id=1, source_target_pairs={{0,2},{1,3},{2,4},{3,5},{4,6},{5,7},{6,0},{7,1},{8,10},{9,11},{10,... | collective-permute-start | bytes 2359304 | tf_op jit(solution)/shard_map/ppermute | solution.py:30
  275.3 18.1 %collective-permute-start.9 = (bf16[768,512]{0,1:T(8,128)(2,1)S(1)}, bf16[768,512]{0,1:T(8,128)(2,1)}, u32[]{:S(2)}, u32[]{:S(2)}) collective-permute-start(bf16[768,512]{0,1:T(8,128)(2,1)S(1)} %get-tuple-element.23), channel_id=1, source_target_pairs={{0,3},{1,4},{2,5},{3,6},{4,7},{5,0},{6,1},{7,2},{8,11},{9,12},{10,... | collective-permute-start | bytes 2359304 | tf_op jit(solution)/shard_map/ppermute | solution.py:30
  293.4 5.8 %fusion.34 = bf16[640,1024]{1,0:T(8,128)(2,1)S(1)} fusion(bf16[2,8,512,1024]{3,2,1,0:T(8,128)(2,1)S(1)} %bitcast.144, bf16[8,768,512]{1,2,0:T(8,128)(2,1)S(1)} %bitcast.138), kind=kOutput, calls=%fused_computation.41 | convolution fusion | flops 5368709120 | bytes 14942208 | tf_op jit(solution)/shard_map/jsc,jch->sh/dot_general | solution.py:102
  299.4 1.3 pad_maximum_fusion.1
  300.7 24.8 %collective-permute-done.7 = bf16[768,512]{0,1:T(8,128)(2,1)} collective-permute-done((bf16[768,512]{0,1:T(8,128)(2,1)S(1)}, bf16[768,512]{0,1:T(8,128)(2,1)}, u32[]{:S(2)}, u32[]{:S(2)}) %collective-permute-start.7) | collective-permute-done | bytes 786464 | tf_op jit(solution)/shard_map/ppermute | solution.py:30
  325.4 24.2 %collective-permute-done.9 = bf16[768,512]{0,1:T(8,128)(2,1)} collective-permute-done((bf16[768,512]{0,1:T(8,128)(2,1)S(1)}, bf16[768,512]{0,1:T(8,128)(2,1)}, u32[]{:S(2)}, u32[]{:S(2)}) %collective-permute-start.9) | collective-permute-done | bytes 786464 | tf_op jit(solution)/shard_map/ppermute | solution.py:30
  349.6 3.1 fusion.51
  352.7 1.2 copy.47
  353.9 26.3 %reduce-scatter.2.cloned.1.call-done = bf16[2,256,1024]{2,1,0:T(8,128)(2,1)} async-done(((bf16[2,4096,1024]{2,1,0:T(8,128)(2,1)}), bf16[2,256,1024]{2,1,0:T(8,128)(2,1)}) %reduce-scatter.2.cloned.1.call-update) | async-done | bytes 1048592 | tf_op jit(solution)/shard_map/reduce_scatter | solution.py:78
  380.2 1.4 fusion.61
  381.6 2.0 copy.48
  (74 shorter events, 2.5 us)
Async XLA Ops:
  7.2 166.4 %all-gather.2.cloned.1.call-start = ((), (), s32[]{:S(2)}) async-start(), calls=%async_computation.1 | async-start | bytes 17825792 | tf_op jit(solution)/shard_map/all_gather | solution.py:52
  7.9 372.3 %reduce-scatter.2.cloned.1.call-start = ((), (), s32[]{:S(2)}) async-start(), calls=%async_computation.2 | async-start | bytes 17825792 | tf_op jit(solution)/shard_map/reduce_scatter | solution.py:78
  9.4 28.2 %collective-permute-start = (bf16[768,512]{0,1:T(8,128)(2,1)S(1)}, bf16[768,512]{0,1:T(8,128)(2,1)S(1)}, u32[]{:S(2)}, u32[]{:S(2)}) collective-permute-start(bf16[768,512]{0,1:T(8,128)(2,1)S(1)} %copy.36), channel_id=1, source_target_pairs={{0,7},{1,0},{2,1},{3,2},{4,3},{5,4},{6,5},{7,6},{8,15},{9,8},{10,9... | collective-permute-start | bytes 2359304 | tf_op jit(solution)/shard_map/ppermute | solution.py:19
  14.9 22.6 %collective-permute-start.1 = (bf16[768,512]{0,1:T(8,128)(2,1)S(1)}, bf16[768,512]{0,1:T(8,128)(2,1)S(1)}, u32[]{:S(2)}, u32[]{:S(2)}) collective-permute-start(bf16[768,512]{0,1:T(8,128)(2,1)S(1)} %copy.36), channel_id=1, source_target_pairs={{0,6},{1,7},{2,0},{3,1},{4,2},{5,3},{6,4},{7,5},{8,14},{9,15},{10,... | collective-permute-start | bytes 2359304 | tf_op jit(solution)/shard_map/ppermute | solution.py:19
  15.1 67.6 %collective-permute-start.2 = (bf16[768,512]{0,1:T(8,128)(2,1)S(1)}, bf16[768,512]{0,1:T(8,128)(2,1)S(1)}, u32[]{:S(2)}, u32[]{:S(2)}) collective-permute-start(bf16[768,512]{0,1:T(8,128)(2,1)S(1)} %copy.36), channel_id=1, source_target_pairs={{0,5},{1,6},{2,7},{3,0},{4,1},{5,2},{6,3},{7,4},{8,13},{9,14},{10,... | collective-permute-start | bytes 2359304 | tf_op jit(solution)/shard_map/ppermute | solution.py:19
  15.1 67.7 %collective-permute-start.3 = (bf16[768,512]{0,1:T(8,128)(2,1)S(1)}, bf16[768,512]{0,1:T(8,128)(2,1)}, u32[]{:S(2)}, u32[]{:S(2)}) collective-permute-start(bf16[768,512]{0,1:T(8,128)(2,1)S(1)} %copy.36), channel_id=1, source_target_pairs={{0,4},{1,5},{2,6},{3,7},{4,0},{5,1},{6,2},{7,3},{8,12},{9,13},{10,... | collective-permute-start | bytes 2359304 | tf_op jit(solution)/shard_map/ppermute | solution.py:19
  18.2 69.1 %collective-permute-start.4 = (bf16[768,512]{0,1:T(8,128)(2,1)S(1)}, bf16[768,512]{0,1:T(8,128)(2,1)}, u32[]{:S(2)}, u32[]{:S(2)}) collective-permute-start(bf16[768,512]{0,1:T(8,128)(2,1)S(1)} %copy.36), channel_id=1, source_target_pairs={{0,3},{1,4},{2,5},{3,6},{4,7},{5,0},{6,1},{7,2},{8,11},{9,12},{10,... | collective-permute-start | bytes 2359304 | tf_op jit(solution)/shard_map/ppermute | solution.py:19
  37.5 51.0 %collective-permute-start.5 = (bf16[768,512]{0,1:T(8,128)(2,1)S(1)}, bf16[768,512]{0,1:T(8,128)(2,1)S(1)}, u32[]{:S(2)}, u32[]{:S(2)}) collective-permute-start(bf16[768,512]{0,1:T(8,128)(2,1)S(1)} %copy.36), channel_id=1, source_target_pairs={{0,2},{1,3},{2,4},{3,5},{4,6},{5,7},{6,0},{7,1},{8,10},{9,11},{10,... | collective-permute-start | bytes 2359304 | tf_op jit(solution)/shard_map/ppermute | solution.py:19
  37.6 83.4 %collective-permute-start.6 = (bf16[768,512]{0,1:T(8,128)(2,1)S(1)}, bf16[768,512]{0,1:T(8,128)(2,1)S(1)}, u32[]{:S(2)}, u32[]{:S(2)}) collective-permute-start(bf16[768,512]{0,1:T(8,128)(2,1)S(1)} %copy.36), channel_id=1, source_target_pairs={{0,1},{1,2},{2,3},{3,4},{4,5},{5,6},{6,7},{7,0},{8,9},{9,10},{10,1... | collective-permute-start | bytes 2359304 | tf_op jit(solution)/shard_map/ppermute | solution.py:19
  121.1 2.8 copy-start.4
  140.9 8.9 %copy-start.5 = (bf16[768,1024]{1,0:T(8,128)(2,1)S(1)}, bf16[768,1024]{1,0:T(8,128)(2,1)}, u32[]{:S(2)}) copy-start(bf16[768,1024]{1,0:T(8,128)(2,1)} %param.7) | copy-start | bytes 4718596
  149.8 9.8 %copy-start.1 = (bf16[640,4096]{0,1:T(8,128)(2,1)S(1)}, bf16[640,4096]{0,1:T(8,128)(2,1)}, u32[]{:S(2)}) copy-start(bf16[640,4096]{0,1:T(8,128)(2,1)} %get-tuple-element.34) | copy-start | bytes 15728644
  213.5 38.0 %slice-start = ((s8[6291456]{0:T(1024)(128)(4,1)}), s8[2097152]{0:T(1024)(128)(4,1)S(1)}, s32[]{:S(2)}) async-start(s8[6291456]{0:T(1024)(128)(4,1)} %bitcast.135), calls=%async_computation.3 | async-start | bytes 4194304
  229.6 22.0 %slice-start.1 = ((s8[6291456]{0:T(1024)(128)(4,1)}), s8[4194304]{0:T(1024)(128)(4,1)S(1)}, s32[]{:S(2)}) async-start(s8[6291456]{0:T(1024)(128)(4,1)} %bitcast.135), calls=%async_computation.4 | async-start | bytes 8388608
  241.6 2.6 copy-start
  244.2 49.2 %slice-start.2 = ((s8[16777216]{0:T(1024)(128)(4,1)}), s8[4194304]{0:T(1024)(128)(4,1)S(1)}, s32[]{:S(2)}) async-start(s8[16777216]{0:T(1024)(128)(4,1)} %bitcast.142), calls=%async_computation.5 | async-start | bytes 8388608
  244.2 49.2 %slice-start.3 = ((s8[16777216]{0:T(1024)(128)(4,1)}), s8[4194304]{0:T(1024)(128)(4,1)S(1)}, s32[]{:S(2)}) async-start(s8[16777216]{0:T(1024)(128)(4,1)} %bitcast.142), calls=%async_computation.6 | async-start | bytes 8388608
  246.7 15.8 %collective-permute-start.10 = (bf16[768,512]{0,1:T(8,128)(2,1)}, bf16[768,512]{0,1:T(8,128)(2,1)S(1)}, u32[]{:S(2)}, u32[]{:S(2)}) collective-permute-start(bf16[768,512]{0,1:T(8,128)(2,1)} %get-tuple-element.22), channel_id=1, source_target_pairs={{0,4},{1,5},{2,6},{3,7},{4,0},{5,1},{6,2},{7,3},{8,12},{9,13},{10,... | collective-permute-start | bytes 2359304 | tf_op jit(solution)/shard_map/ppermute | solution.py:30
  246.7 28.6 %collective-permute-start.11 = (bf16[768,512]{0,1:T(8,128)(2,1)}, bf16[768,512]{0,1:T(8,128)(2,1)S(1)}, u32[]{:S(2)}, u32[]{:S(2)}) collective-permute-start(bf16[768,512]{0,1:T(8,128)(2,1)} %get-tuple-element.21), channel_id=1, source_target_pairs={{0,5},{1,6},{2,7},{3,0},{4,1},{5,2},{6,3},{7,4},{8,13},{9,14},{10,... | collective-permute-start | bytes 2359304 | tf_op jit(solution)/shard_map/ppermute | solution.py:30
  251.6 8.8 %copy-start.3 = (bf16[768,512]{0,1:T(8,128)(2,1)S(1)}, bf16[768,512]{0,1:T(8,128)(2,1)}, u32[]{:S(2)}) copy-start(bf16[768,512]{0,1:T(8,128)(2,1)} %get-tuple-element.18) | copy-start | bytes 2359300
  251.6 10.9 %copy-start.2 = (bf16[768,512]{0,1:T(8,128)(2,1)S(1)}, bf16[768,512]{0,1:T(8,128)(2,1)}, u32[]{:S(2)}) copy-start(bf16[768,512]{0,1:T(8,128)(2,1)} %get-tuple-element.24) | copy-start | bytes 2359300
  251.6 41.8 %slice-start.4 = ((s8[16777216]{0:T(1024)(128)(4,1)}), s8[4194304]{0:T(1024)(128)(4,1)S(1)}, s32[]{:S(2)}) async-start(s8[16777216]{0:T(1024)(128)(4,1)} %bitcast.142), calls=%async_computation.7 | async-start | bytes 8388608
  251.6 41.8 %slice-start.5 = ((s8[16777216]{0:T(1024)(128)(4,1)}), s8[4194304]{0:T(1024)(128)(4,1)S(1)}, s32[]{:S(2)}) async-start(s8[16777216]{0:T(1024)(128)(4,1)} %bitcast.142), calls=%async_computation.8 | async-start | bytes 8388608
  260.1 40.6 %collective-permute-start.12 = (bf16[768,512]{0,1:T(8,128)(2,1)}, bf16[768,512]{0,1:T(8,128)(2,1)}, u32[]{:S(2)}, u32[]{:S(2)}) collective-permute-start(bf16[768,512]{0,1:T(8,128)(2,1)} %get-tuple-element.20), channel_id=1, source_target_pairs={{0,6},{1,7},{2,0},{3,1},{4,2},{5,3},{6,4},{7,5},{8,14},{9,15},{10,... | collective-permute-start | bytes 2359304 | tf_op jit(solution)/shard_map/ppermute | solution.py:30
  260.2 40.5 %collective-permute-start.13 = (bf16[768,512]{0,1:T(8,128)(2,1)}, bf16[768,512]{0,1:T(8,128)(2,1)}, u32[]{:S(2)}, u32[]{:S(2)}) collective-permute-start(bf16[768,512]{0,1:T(8,128)(2,1)} %get-tuple-element.19), channel_id=1, source_target_pairs={{0,7},{1,0},{2,1},{3,2},{4,3},{5,4},{6,5},{7,6},{8,15},{9,8},{10,9... | collective-permute-start | bytes 2359304 | tf_op jit(solution)/shard_map/ppermute | solution.py:30
  260.3 65.1 %collective-permute-start.7 = (bf16[768,512]{0,1:T(8,128)(2,1)S(1)}, bf16[768,512]{0,1:T(8,128)(2,1)}, u32[]{:S(2)}, u32[]{:S(2)}) collective-permute-start(bf16[768,512]{0,1:T(8,128)(2,1)S(1)} %copy-done.3), channel_id=1, source_target_pairs={{0,1},{1,2},{2,3},{3,4},{4,5},{5,6},{6,7},{7,0},{8,9},{9,10},{10,1... | collective-permute-start | bytes 2359304 | tf_op jit(solution)/shard_map/ppermute | solution.py:30
  262.5 62.9 %collective-permute-start.8 = (bf16[768,512]{0,1:T(8,128)(2,1)S(1)}, bf16[768,512]{0,1:T(8,128)(2,1)}, u32[]{:S(2)}, u32[]{:S(2)}) collective-permute-start(bf16[768,512]{0,1:T(8,128)(2,1)S(1)} %copy-done.2), channel_id=1, source_target_pairs={{0,2},{1,3},{2,4},{3,5},{4,6},{5,7},{6,0},{7,1},{8,10},{9,11},{10,... | collective-permute-start | bytes 2359304 | tf_op jit(solution)/shard_map/ppermute | solution.py:30
  275.3 74.3 %collective-permute-start.9 = (bf16[768,512]{0,1:T(8,128)(2,1)S(1)}, bf16[768,512]{0,1:T(8,128)(2,1)}, u32[]{:S(2)}, u32[]{:S(2)}) collective-permute-start(bf16[768,512]{0,1:T(8,128)(2,1)S(1)} %get-tuple-element.23), channel_id=1, source_target_pairs={{0,3},{1,4},{2,5},{3,6},{4,7},{5,0},{6,1},{7,2},{8,11},{9,12},{10,... | collective-permute-start | bytes 2359304 | tf_op jit(solution)/shard_map/ppermute | solution.py:30
Sparse Core Ops, SparseCore 0:
  10.5 151.8 all-gather.1
  190.2 189.9 reduce-scatter.1

commit v3 on v2

--- a/solution.py
+++ b/solution.py
@@ -49,9 +49,14 @@
     slot_scale = combine_weight * live.astype(jnp.float32)
     slot_expert = jnp.repeat(block_expert, BLK)
 
-    panel = lax.all_gather(jnp.transpose(down_weight, (1, 0, 2)), "fsdp", axis=1, tiled=True)
-    model_width = panel.shape[1]
-    panel_parts = panel.reshape(EXPERTS, n_dp, part_width, hidden_width)
+    n_core = lax.axis_size("core")
+    core = lax.axis_index("core")
+    own = lax.all_gather(jnp.transpose(down_weight, (1, 0, 2)), "fo", axis=1, tiled=False)
+    other = lax.ppermute(own, "core", ring_pairs(n_core, 1))
+    both = jnp.stack([own, other, own], axis=2)
+    panel = lax.dynamic_slice_in_dim(both, core, n_core, axis=2)
+    model_width = panel.shape[1] * panel.shape[2] * panel.shape[3]
+    panel_parts = panel.reshape(EXPERTS, n_dp, model_width // n_dp, hidden_width)
 
     full_cot = gather_major(cotangent, "dp")
     tok_hot = (slot_token[:, None] == positions[None, :]).astype(jnp.bfloat16)
@@ -75,10 +80,16 @@
         )
     device_grad = jnp.stack(grads, axis=0)
     device_grad, panel_parts = lax.optimization_barrier((device_grad, panel_parts))
-    summed = lax.psum_scatter(device_grad, "fsdp", scatter_dimension=1, tiled=True).astype(
+    n_fo = lax.axis_size("fo")
+    split = device_grad.reshape(EXPERTS, n_fo, n_core, model_width // (n_fo * n_core), hidden_width)
+    keep = lax.dynamic_index_in_dim(split, core, axis=2, keepdims=False)
+    send = lax.dynamic_index_in_dim(split, (core + 1) % n_core, axis=2, keepdims=False)
+    pair_sum = keep.astype(jnp.float32) + lax.ppermute(send, "core", ring_pairs(n_core, 1)).astype(
         jnp.float32
     )
-    grad_scale = 1.0 / math.sqrt(lax.axis_size("fsdp") * slot_count)
+    summed = lax.psum_scatter(pair_sum.astype(jnp.bfloat16), "fo", scatter_dimension=1, tiled=True)
+    grad_scale = 1.0 / math.sqrt(lax.axis_size(("fo", "core")) * slot_count)
+    summed = summed.reshape(EXPERTS, -1, hidden_width).astype(jnp.float32)
     grad_down = jnp.transpose((summed * grad_scale).astype(jnp.bfloat16), (1, 0, 2))
 
     combined = None
@@ -111,14 +122,19 @@
 
 
 def solution(mesh):
+    n_fsdp = mesh.shape["fsdp"]
+    n_core = 2
+    devices = mesh.devices.reshape(n_fsdp // n_core, n_core, mesh.shape["dp"])
+    fine = jax.sharding.Mesh(devices, ("fo", "core", "dp"))
+    rows = ("fo", "core")
     in_specs = (
-        P("fsdp", "dp"),
-        P("fsdp"),
-        P("fsdp", None, "dp"),
-        P("fsdp", "dp"),
-        P("fsdp", None),
-        P("fsdp"),
-        P("fsdp"),
+        P(rows, "dp"),
+        P(rows),
+        P(rows, None, "dp"),
+        P(rows, "dp"),
+        P(rows, None),
+        P(rows),
+        P(rows),
     )
-    out_specs = (P("fsdp", "dp"), P("fsdp", "dp"), P("fsdp", None, "dp"))
-    return jax.shard_map(local, mesh=mesh, in_specs=in_specs, out_specs=out_specs, check_vma=False)
+    out_specs = (P(rows, "dp"), P(rows, "dp"), P(rows, None, "dp"))
+    return jax.shard_map(local, mesh=fine, in_specs=in_specs, out_specs=out_specs, check_vma=False)

time: 395 us -> 466 us (1.18)
  local copies, waits for them, and re-layouts: 63.4 us -> 94.3 us
  other arithmetic: 25.2 us -> 53.7 us
  waiting for transfers between devices: 126 us -> 147 us
  starting transfers between devices: 91.3 us -> 77.2 us
    all_gather x1, waiting for transfers between devices: 0.01 us -> 34.5 us  [local(): lax.all_gather(jnp.transpose(down_weight, (1, 0, 2)), 'fo', axis=1, tiled...]
    reduce_scatter x1, waiting for transfers between devices: 26.3 us -> 0.01 us  [local(): lax.psum_scatter(pair_sum.astype(jnp.bfloat16), 'fo', scatter_dimension=1...]
    another operation x1 -> x2, other arithmetic: 0.17 us -> 19.6 us  [the longest x1 19.4 us: local(): both = jnp.stack([own, other, own], axis=2)]
    ppermute x7, starting transfers between devices: 37.4 us -> 22.1 us  [scatter_sum_major(): lax.ppermute(piece, axis_name, ring_pairs(n, k)).astype(jnp.float32)]
    dynamic_slice x0 -> x2, local copies, waits for them, and re-layouts: none -> 14.3 us  [the longest x1 8.07 us: local(): lax.dynamic_index_in_dim(split, (core + 1) % n_core, axis=2, keepdims=False)]
    unnamed x42 -> x58, local copies, waits for them, and re-layouts: 12.6 us -> 26.2 us
    ppermute x0 -> x2, waiting for transfers between devices: none -> 13 us  [the longest x1 13 us: local(): lax.ppermute(send, 'core', ring_pairs(n_core, 1)).astype(jnp.float32)]
    another operation x1 -> x2, local copies, waits for them, and re-layouts: 0.01 us -> 9.4 us  [the longest x1 9.39 us: local(): both = jnp.stack([own, other, own], axis=2)]
  transfers between devices with their start and end apart: 16 -> 18, of which waited for: 7 -> 10; matrix products, arithmetic and copies ran while one was open for 35% -> 35% of each run, Pallas kernels for 0% -> 0%
where the time goes in v3:
time: 466 us; the launch traced here: 461 us
  waiting for transfers between devices  147 us (32%)
  local copies, waits for them, and re-layouts  94.3 us (20%)
  starting transfers between devices  77.2 us (17%)
  matrix products  72 us (15%)
  other arithmetic  53.7 us (12%)
  between operations  16.2 us (3%)
    ppermute x7, waiting for transfers between devices, scatter_sum_major(): lax.ppermute(piece, axis_name, ring_pairs(n, k)).astype(jnp.float32)  54.5 us
    ppermute x7, starting transfers between devices, gather_major(): lax.ppermute(piece, axis_name, ring_pairs(n, k))  51.7 us
    ppermute x7, waiting for transfers between devices, gather_major(): lax.ppermute(piece, axis_name, ring_pairs(n, k))  44.8 us
    all_gather x1, waiting for transfers between devices, local(): lax.all_gather(jnp.transpose(down_weight, (1, 0, 2)), 'fo', axis=1, tiled...  34.5 us
    dot_general x2, matrix products, local(): jnp.einsum('th,jch->jtc', hid_e, panel_parts[e], preferred_element_type=j...  27.3 us
    unnamed x58, local copies, waits for them, and re-layouts  26.2 us
    ppermute x7, starting transfers between devices, scatter_sum_major(): lax.ppermute(piece, axis_name, ring_pairs(n, k)).astype(jnp.float32)  22.1 us
    another operation x1, other arithmetic, local(): both = jnp.stack([own, other, own], axis=2)  19.4 us
  transfers between devices with their start and end apart: 18, of which 10 were waited for; matrix products, arithmetic and copies ran while one was open for 35% of the time, Pallas kernels for 0%

profile of v3, /device:TPU:1, one launch (start us, length us, event | category | flops | bytes accessed | tf_op | source)
XLA Modules:
  0.0 460.8 jit_solution(17527438625996878174)
XLA Ops:
  9.4 5.6 %collective-permute-start = (bf16[768,512]{0,1:T(8,128)(2,1)S(1)}, bf16[768,512]{0,1:T(8,128)(2,1)}, u32[]{:S(2)}, u32[]{:S(2)}) collective-permute-start(bf16[768,512]{0,1:T(8,128)(2,1)S(1)} %copy.42), channel_id=1, source_target_pairs={{0,7},{1,0},{2,1},{3,2},{4,3},{5,4},{6,5},{7,6},{8,15},{9,8},{10,9... | collective-permute-start | bytes 2359304 | tf_op jit(solution)/shard_map/ppermute | solution.py:19
  15.1 3.1 collective-permute-start.3
  21.5 2.1 compare_select_fusion.3
  25.4 12.2 %collective-permute-done = bf16[768,512]{0,1:T(8,128)(2,1)} collective-permute-done((bf16[768,512]{0,1:T(8,128)(2,1)S(1)}, bf16[768,512]{0,1:T(8,128)(2,1)}, u32[]{:S(2)}, u32[]{:S(2)}) %collective-permute-start) | collective-permute-done | bytes 786464 | tf_op jit(solution)/shard_map/ppermute | solution.py:19
  37.6 2.1 bitcast_dynamic-update-slice_fusion.12
  39.7 42.9 %collective-permute-start.6 = (bf16[768,512]{0,1:T(8,128)(2,1)S(1)}, bf16[768,512]{0,1:T(8,128)(2,1)S(1)}, u32[]{:S(2)}, u32[]{:S(2)}) collective-permute-start(bf16[768,512]{0,1:T(8,128)(2,1)S(1)} %copy.42), channel_id=1, source_target_pairs={{0,1},{1,2},{2,3},{3,4},{4,5},{5,6},{6,7},{7,0},{8,9},{9,10},{10,1... | collective-permute-start | bytes 2359304 | tf_op jit(solution)/shard_map/ppermute | solution.py:19
  85.4 2.0 collective-permute-done.4
  87.5 2.1 bitcast_dynamic-update-slice_fusion.4
  90.6 30.6 %collective-permute-done.6 = bf16[768,512]{0,1:T(8,128)(2,1)S(1)} collective-permute-done((bf16[768,512]{0,1:T(8,128)(2,1)S(1)}, bf16[768,512]{0,1:T(8,128)(2,1)S(1)}, u32[]{:S(2)}, u32[]{:S(2)}) %collective-permute-start.6) | collective-permute-done | bytes 786464 | tf_op jit(solution)/shard_map/ppermute | solution.py:19
  123.1 2.1 bitcast_dynamic-update-slice_fusion.13
  125.2 34.5 %all-gather.3.cloned.1.call-done = bf16[2,2048,1024]{2,0,1:T(2,128)(2,1)} async-done(((bf16[2,256,1024]{2,0,1:T(2,128)(2,1)}), bf16[2,2048,1024]{2,0,1:T(2,128)(2,1)}) %all-gather.3.cloned.1.call-update) | async-done | bytes 8388624 | tf_op jit(solution)/shard_map/all_gather | solution.py:54
  159.7 9.6 %copy.50 = bf16[2,8,256,1024]{3,2,1,0:T(8,128)(2,1)} copy(bf16[2,8,256,1024]{3,0,2,1:T(2,128)(2,1)} %bitcast.151) | data formatting | bytes 16777216 | tf_op jit(solution)/shard_map/all_gather | solution.py:54
  173.4 2.1 bitcast_dynamic-update-slice_fusion.5
  177.4 10.3 %multiply_convert_fusion = bf16[8,512,768]{2,1,0:T(8,128)(2,1)} fusion(f32[768]{0:T(1024)S(1)} %broadcast_select_fusion.2, bf16[16,768,512]{1,2,0:T(8,128)(2,1)} %bitcast_dynamic-update-slice_fusion.1, s32[]{:T(128)S(6)} %select_n.143, s32[768]{0:T(1024)S(1)} %copy-done.8), kind=kOutput, calls=%fused_computation.15 | convolution fusion | flops 4838719488 | bytes 12589060 | tf_op jit(solution)/shard_map/st,jtc->jsc/dot_general | solution.py:63
  187.6 9.6 %fusion.86 = (bf16[640,8,512]{0,2,1:T(8,128)(2,1)}, bf16[640,8,512]{0,2,1:T(8,128)(2,1)}) fusion(bf16[768,8,512]{0,2,1:T(8,128)(2,1)} %bitcast.153), kind=kLoop, calls=%fused_computation.137 | loop fusion | bytes 20971520 | tf_op jit(solution)/shard_map/slice | solution.py:74
  197.2 9.0 %bitcast_select_fusion = (bf16[640,4096]{0,1:T(8,128)(2,1)}, bf16[640,4096]{0,1:T(8,128)(2,1)}) fusion(bf16[640,8,512]{0,2,1:T(8,128)(2,1)} %get-tuple-element.28, pred[640]{0:T(1024)(128)(4,1)S(1)} %broadcast_bitcast_fusion, bf16[640,8,512]{0,2,1:T(8,128)(2,1)} %get-tuple-element.27, pred[640]{0:T(1024)(128)(4,1)S(1)} %broadcast_bitcast_fusion.1), kind=kLoop, calls=%fused_computation.36 | loop fusion | flops 5242880 | bytes 20972800 | tf_op jit(solution)/shard_map/jit(_where)/select_n | solution.py:75
  206.2 9.5 %convert_bitcast_fusion = bf16[1,4096,1024]{2,1,0:T(8,128)(2,1)S(1)} fusion(bf16[640,4096]{0,1:T(8,128)(2,1)} %get-tuple-element.35, bf16[768,1024]{1,0:T(8,128)(2,1)S(1)} %copy-done.9), kind=kOutput, calls=%fused_computation.26 | convolution fusion | flops 5372903424 | bytes 14942208 | tf_op jit(solution)/shard_map/sd,sh->dh/dot_general | solution.py:77
  215.7 7.1 %convert_bitcast_fusion.1 = bf16[1,4096,1024]{2,1,0:T(8,128)(2,1)S(1)} fusion(bf16[640,4096]{0,1:T(8,128)(2,1)S(1)} %copy-done.1, bf16[768,1024]{1,0:T(8,128)(2,1)S(1)} %copy-done.9), kind=kOutput, calls=%fused_computation.27 | convolution fusion | flops 5372903424 | bytes 14942208 | tf_op jit(solution)/shard_map/sd,sh->dh/dot_general | solution.py:77
  222.9 6.7 %pad_maximum_fusion = bf16[2,4096,1024]{2,1,0:T(8,128)(2,1)} fusion(bf16[1,4096,1024]{2,1,0:T(8,128)(2,1)S(1)} %convert_bitcast_fusion, bf16[1,4096,1024]{2,1,0:T(8,128)(2,1)S(1)} %convert_bitcast_fusion.1), kind=kLoop, calls=%fused_computation.11 | loop fusion | flops 8388608 | bytes 33554432 | tf_op jit(solution)/shard_map/stack | solution.py:81
  229.6 9.4 %copy.51 = bf16[2,8,1,256,1024]{4,3,2,1,0:T(8,128)(2,1)} copy(bf16[2,8,1,256,1024]{4,0,3,1,2:T(2,128)(2,1)} %bitcast.152) | data formatting | bytes 16777216 | tf_op jit(solution)/shard_map/stack | solution.py:56
  239.0 19.4 %fusion.1 = bf16[2,8,2,256,1024]{4,3,2,1,0:T(8,128)(2,1)} fusion(s32[]{:T(128)S(6)} %select_n.146, bf16[2,8,1,256,1024]{4,3,2,1,0:T(8,128)(2,1)} %copy.51, bf16[2,8,1,256,1024]{4,3,2,1,0:T(8,128)(2,1)} %bitcast.22), kind=kLoop, calls=%fused_computation.10 | loop fusion | flops 16777216 | bytes 33554436 | tf_op jit(solution)/shard_map/stack | solution.py:56
  258.5 6.3 %constant_dynamic-slice_fusion.1 = (bf16[2,8,1,256,1024]{4,3,2,1,0:T(8,128)(2,1)}, bf16[2,8,1,256,1024]{4,3,2,1,0:T(8,128)(2,1)}) fusion(bf16[2,8,2,256,1024]{4,3,2,1,0:T(8,128)(2,1)S(1)} %bitcast.150, s32[]{:T(128)S(6)} %select_n.167, s32[]{:T(128)S(6)} %select_n.169), kind=kLoop, calls=%fused_computation.119 | loop fusion | bytes 33554440 | tf_op jit(solution)/shard_map/jit(dynamic_index_in_dim)/dynamic_slice | solution.py:85
  264.7 8.1 %copy.66 = bf16[2,8,1,256,1024]{4,3,0,1,2:T(8,128)(2,1)} copy(bf16[2,8,1,256,1024]{4,3,2,1,0:T(8,128)(2,1)} %get-tuple-element.19) | data formatting | bytes 16777216 | tf_op jit(solution)/shard_map/jit(dynamic_index_in_dim)/dynamic_slice | solution.py:86
  272.8 2.0 collective-permute-start.15
  274.8 13.0 %collective-permute-done.15 = bf16[2,8,256,1024]{3,2,0,1:T(8,128)(2,1)S(1)} collective-permute-done((bf16[2,8,256,1024]{3,2,0,1:T(8,128)(2,1)}, bf16[2,8,256,1024]{3,2,0,1:T(8,128)(2,1)S(1)}, u32[]{:S(2)}, u32[]{:S(2)}) %collective-permute-start.15) | collective-permute-done | bytes 8388640 | tf_op jit(solution)/shard_map/ppermute | solution.py:87
  287.8 9.0 %fusion.2 = bf16[2,8,256,1024]{3,2,0,1:T(8,128)(2,1)} fusion(bf16[2,8,256,1024]{3,2,0,1:T(8,128)(2,1)S(1)} %collective-permute-done.15, bf16[2,8,1,256,1024]{4,3,2,1,0:T(8,128)(2,1)} %get-tuple-element.18), kind=kLoop, calls=%fused_computation.13 | loop fusion | flops 16777216 | bytes 25165824 | tf_op jit(solution)/shard_map/convert_element_type | solution.py:90
  297.0 3.4 scatter_custom_fusion.3
  300.4 3.4 scatter_custom_fusion.2
  303.8 3.4 scatter_custom_fusion
  307.2 3.4 scatter_custom_fusion.1
  310.6 3.4 gather_fusion.1
  314.0 3.2 gather_fusion
  317.4 2.6 fusion.45
  319.9 15.0 %fusion.5 = f32[8,512,768]{2,1,0:T(8,128)} fusion(bf16[2,8,512,1024]{3,2,1,0:T(8,128)(2,1)} %bitcast.158, bf16[768,1024]{1,0:T(8,128)(2,1)} %param.7, s32[768]{0:T(1024)S(1)} %scatter_custom_fusion.3, pred[768]{0:T(1024)(128)(4,1)S(1)} %scatter_custom_fusion.2), kind=kOutput, calls=%fused_computation.19 | convolution fusion | flops 7652376576 | bytes 22548224 | tf_op jit(solution)/shard_map/th,jch->jtc/dot_general | solution.py:104
  334.9 12.4 %add_convert_fusion = bf16[8,512,768]{2,1,0:T(8,128)(2,1)S(1)} fusion(f32[8,512,768]{2,1,0:T(8,128)} %fusion.5, f32[768]{0:T(1024)S(1)} %broadcast_select_fusion, f32[768]{0:T(1024)S(1)} %broadcast_select_fusion.1, bf16[2,8,512,1024]{3,2,1,0:T(8,128)(2,1)} %bitcast.159, bf16[768,1024]{1,0:T(8,128)(2,1)} %fusion.45), kind=kOutput, calls=%fused_computation.14 | convolution fusion | flops 6455033856 | bytes 28841984 | tf_op jit(solution)/shard_map/th,jch->jtc/dot_general | solution.py:104
  347.3 2.6 copy-done
  349.9 2.5 dynamic-slice_bitcast_fusion.6
  352.5 9.4 %fusion.32 = bf16[640,1024]{1,0:T(8,128)(2,1)S(1)} fusion(bf16[2,8,512,1024]{3,2,1,0:T(8,128)(2,1)} %bitcast.160, bf16[8,768,512]{1,2,0:T(8,128)(2,1)S(1)} %bitcast.156), kind=kOutput, calls=%fused_computation.49 | convolution fusion | flops 5368709120 | bytes 14942208 | tf_op jit(solution)/shard_map/jsc,jch->sh/dot_general | solution.py:113
  361.8 3.2 collective-permute-start.12
  366.8 18.8 %collective-permute-done.10 = bf16[768,512]{0,1:T(8,128)(2,1)S(1)} collective-permute-done((bf16[768,512]{0,1:T(8,128)(2,1)}, bf16[768,512]{0,1:T(8,128)(2,1)S(1)}, u32[]{:S(2)}, u32[]{:S(2)}) %collective-permute-start.10) | collective-permute-done | bytes 786464 | tf_op jit(solution)/shard_map/ppermute | solution.py:30
  385.6 4.3 collective-permute-done.11
  389.9 17.2 %collective-permute-start.9 = (bf16[768,512]{0,1:T(8,128)(2,1)S(1)}, bf16[768,512]{0,1:T(8,128)(2,1)}, u32[]{:S(2)}, u32[]{:S(2)}) collective-permute-start(bf16[768,512]{0,1:T(8,128)(2,1)S(1)} %get-tuple-element.26), channel_id=1, source_target_pairs={{0,2},{1,3},{2,4},{3,5},{4,6},{5,7},{6,0},{7,1},{8,10},{9,11},{10,... | collective-permute-start | bytes 2359304 | tf_op jit(solution)/shard_map/ppermute | solution.py:30
  407.1 5.8 %fusion.37 = bf16[640,1024]{1,0:T(8,128)(2,1)S(1)} fusion(bf16[2,8,512,1024]{3,2,1,0:T(8,128)(2,1)S(1)} %bitcast.163, bf16[8,768,512]{1,2,0:T(8,128)(2,1)S(1)} %bitcast.157), kind=kOutput, calls=%fused_computation.50 | convolution fusion | flops 5368709120 | bytes 14942208 | tf_op jit(solution)/shard_map/jsc,jch->sh/dot_general | solution.py:113
  414.3 6.4 %collective-permute-done.13 = bf16[768,512]{0,1:T(8,128)(2,1)} collective-permute-done((bf16[768,512]{0,1:T(8,128)(2,1)}, bf16[768,512]{0,1:T(8,128)(2,1)}, u32[]{:S(2)}, u32[]{:S(2)}) %collective-permute-start.13) | collective-permute-done | bytes 786464 | tf_op jit(solution)/shard_map/ppermute | solution.py:30
  420.7 4.8 %collective-permute-done.14 = bf16[768,512]{0,1:T(8,128)(2,1)} collective-permute-done((bf16[768,512]{0,1:T(8,128)(2,1)S(1)}, bf16[768,512]{0,1:T(8,128)(2,1)}, u32[]{:S(2)}, u32[]{:S(2)}) %collective-permute-start.14) | collective-permute-done | bytes 786464 | tf_op jit(solution)/shard_map/ppermute | solution.py:30
  425.6 20.2 %collective-permute-done.8 = bf16[768,512]{0,1:T(8,128)(2,1)} collective-permute-done((bf16[768,512]{0,1:T(8,128)(2,1)S(1)}, bf16[768,512]{0,1:T(8,128)(2,1)}, u32[]{:S(2)}, u32[]{:S(2)}) %collective-permute-start.8) | collective-permute-done | bytes 786464 | tf_op jit(solution)/shard_map/ppermute | solution.py:30
  445.8 3.1 fusion.54
  451.5 2.0 copy.58
  (100 shorter events, 24.1 us)
Async XLA Ops:
  7.2 152.5 %all-gather.3.cloned.1.call-start = ((), (), s32[]{:S(2)}) async-start(), calls=%async_computation.2 | async-start | bytes 9437184 | tf_op jit(solution)/shard_map/all_gather | solution.py:54
  7.9 442.2 %reduce-scatter.2.cloned.1.call-start = ((), (), s32[]{:S(2)}) async-start(), calls=%async_computation.1 | async-start | bytes 9437184 | tf_op jit(solution)/shard_map/reduce_scatter | solution.py:90
  9.4 28.3 %collective-permute-start = (bf16[768,512]{0,1:T(8,128)(2,1)S(1)}, bf16[768,512]{0,1:T(8,128)(2,1)}, u32[]{:S(2)}, u32[]{:S(2)}) collective-permute-start(bf16[768,512]{0,1:T(8,128)(2,1)S(1)} %copy.42), channel_id=1, source_target_pairs={{0,7},{1,0},{2,1},{3,2},{4,3},{5,4},{6,5},{7,6},{8,15},{9,8},{10,9... | collective-permute-start | bytes 2359304 | tf_op jit(solution)/shard_map/ppermute | solution.py:19
  14.9 24.8 %collective-permute-start.1 = (bf16[768,512]{0,1:T(8,128)(2,1)S(1)}, bf16[768,512]{0,1:T(8,128)(2,1)S(1)}, u32[]{:S(2)}, u32[]{:S(2)}) collective-permute-start(bf16[768,512]{0,1:T(8,128)(2,1)S(1)} %copy.42), channel_id=1, source_target_pairs={{0,6},{1,7},{2,0},{3,1},{4,2},{5,3},{6,4},{7,5},{8,14},{9,15},{10,... | collective-permute-start | bytes 2359304 | tf_op jit(solution)/shard_map/ppermute | solution.py:19
  15.1 68.5 %collective-permute-start.2 = (bf16[768,512]{0,1:T(8,128)(2,1)S(1)}, bf16[768,512]{0,1:T(8,128)(2,1)S(1)}, u32[]{:S(2)}, u32[]{:S(2)}) collective-permute-start(bf16[768,512]{0,1:T(8,128)(2,1)S(1)} %copy.42), channel_id=1, source_target_pairs={{0,5},{1,6},{2,7},{3,0},{4,1},{5,2},{6,3},{7,4},{8,13},{9,14},{10,... | collective-permute-start | bytes 2359304 | tf_op jit(solution)/shard_map/ppermute | solution.py:19
  15.1 69.4 %collective-permute-start.3 = (bf16[768,512]{0,1:T(8,128)(2,1)S(1)}, bf16[768,512]{0,1:T(8,128)(2,1)S(1)}, u32[]{:S(2)}, u32[]{:S(2)}) collective-permute-start(bf16[768,512]{0,1:T(8,128)(2,1)S(1)} %copy.42), channel_id=1, source_target_pairs={{0,4},{1,5},{2,6},{3,7},{4,0},{5,1},{6,2},{7,3},{8,12},{9,13},{10,... | collective-permute-start | bytes 2359304 | tf_op jit(solution)/shard_map/ppermute | solution.py:19
  18.2 69.3 %collective-permute-start.4 = (bf16[768,512]{0,1:T(8,128)(2,1)S(1)}, bf16[768,512]{0,1:T(8,128)(2,1)}, u32[]{:S(2)}, u32[]{:S(2)}) collective-permute-start(bf16[768,512]{0,1:T(8,128)(2,1)S(1)} %copy.42), channel_id=1, source_target_pairs={{0,3},{1,4},{2,5},{3,6},{4,7},{5,0},{6,1},{7,2},{8,11},{9,12},{10,... | collective-permute-start | bytes 2359304 | tf_op jit(solution)/shard_map/ppermute | solution.py:19
  37.6 51.9 %collective-permute-start.5 = (bf16[768,512]{0,1:T(8,128)(2,1)S(1)}, bf16[768,512]{0,1:T(8,128)(2,1)S(1)}, u32[]{:S(2)}, u32[]{:S(2)}) collective-permute-start(bf16[768,512]{0,1:T(8,128)(2,1)S(1)} %copy.42), channel_id=1, source_target_pairs={{0,2},{1,3},{2,4},{3,5},{4,6},{5,7},{6,0},{7,1},{8,10},{9,11},{10,... | collective-permute-start | bytes 2359304 | tf_op jit(solution)/shard_map/ppermute | solution.py:19
  39.7 81.5 %collective-permute-start.6 = (bf16[768,512]{0,1:T(8,128)(2,1)S(1)}, bf16[768,512]{0,1:T(8,128)(2,1)S(1)}, u32[]{:S(2)}, u32[]{:S(2)}) collective-permute-start(bf16[768,512]{0,1:T(8,128)(2,1)S(1)} %copy.42), channel_id=1, source_target_pairs={{0,1},{1,2},{2,3},{3,4},{4,5},{5,6},{6,7},{7,0},{8,9},{9,10},{10,1... | collective-permute-start | bytes 2359304 | tf_op jit(solution)/shard_map/ppermute | solution.py:19
  89.6 33.6 %copy-start.2 = (bf16[768,512]{0,1:T(8,128)(2,1)}, bf16[768,512]{0,1:T(8,128)(2,1)S(1)}, u32[]{:S(2)}) copy-start(bf16[768,512]{0,1:T(8,128)(2,1)S(1)} %collective-permute-done.5) | copy-start | bytes 2359300
  121.2 2.0 copy-start.4
  159.7 15.8 %copy-start.3 = (bf16[768,512]{0,1:T(8,128)(2,1)S(1)}, bf16[768,512]{0,1:T(8,128)(2,1)}, u32[]{:S(2)}) copy-start(bf16[768,512]{0,1:T(8,128)(2,1)} %copy-done.2) | copy-start | bytes 2359300
  159.7 16.8 %copy-start.5 = (bf16[768,512]{0,1:T(8,128)(2,1)S(1)}, bf16[768,512]{0,1:T(8,128)(2,1)}, u32[]{:S(2)}) copy-start(bf16[768,512]{0,1:T(8,128)(2,1)} %copy-done.4) | copy-start | bytes 2359300
  169.3 8.1 %copy-start.8 = (s32[768]{0:T(1024)S(1)}, s32[768]{0:T(1024)}, u32[]{:S(2)}) copy-start(s32[768]{0:T(1024)} %param.13) | copy-start | bytes 9220
  169.3 69.7 %collective-permute-start.7 = (bf16[2,8,256,1024]{3,2,1,0:T(8,128)(2,1)}, bf16[2,8,256,1024]{3,2,1,0:T(8,128)(2,1)}, u32[]{:S(2)}, u32[]{:S(2)}) collective-permute-start(bf16[2,8,256,1024]{3,2,1,0:T(8,128)(2,1)} %copy.50), channel_id=1, source_target_pairs={{0,8},{8,0},{1,9},{9,1},{2,10},{10,2},{3,11},{11,3},{4,12},{12,4},... | collective-permute-start | bytes 25165832 | tf_op jit(solution)/shard_map/ppermute | solution.py:55
  197.2 9.0 %copy-start.9 = (bf16[768,1024]{1,0:T(8,128)(2,1)S(1)}, bf16[768,1024]{1,0:T(8,128)(2,1)}, u32[]{:S(2)}) copy-start(bf16[768,1024]{1,0:T(8,128)(2,1)} %param.7) | copy-start | bytes 4718596
  206.2 9.6 %copy-start.1 = (bf16[640,4096]{0,1:T(8,128)(2,1)S(1)}, bf16[640,4096]{0,1:T(8,128)(2,1)}, u32[]{:S(2)}) copy-start(bf16[640,4096]{0,1:T(8,128)(2,1)} %get-tuple-element.36) | copy-start | bytes 15728644
  239.0 19.4 %slice-start = ((s8[16777216]{0:T(1024)(128)(4,1)}), s8[4194304]{0:T(1024)(128)(4,1)S(1)}, s32[]{:S(2)}) async-start(s8[16777216]{0:T(1024)(128)(4,1)} %bitcast.148), calls=%async_computation.3 | async-start | bytes 8388608
  239.0 19.4 %slice-start.1 = ((s8[16777216]{0:T(1024)(128)(4,1)}), s8[4194304]{0:T(1024)(128)(4,1)S(1)}, s32[]{:S(2)}) async-start(s8[16777216]{0:T(1024)(128)(4,1)} %bitcast.148), calls=%async_computation.4 | async-start | bytes 8388608
  239.0 19.4 %slice-start.2 = ((s8[16777216]{0:T(1024)(128)(4,1)}), s8[4194304]{0:T(1024)(128)(4,1)S(1)}, s32[]{:S(2)}) async-start(s8[16777216]{0:T(1024)(128)(4,1)} %bitcast.148), calls=%async_computation.5 | async-start | bytes 8388608
  239.0 19.4 %slice-start.3 = ((s8[16777216]{0:T(1024)(128)(4,1)}), s8[4194304]{0:T(1024)(128)(4,1)S(1)}, s32[]{:S(2)}) async-start(s8[16777216]{0:T(1024)(128)(4,1)} %bitcast.148), calls=%async_computation.6 | async-start | bytes 8388608
  272.8 15.0 %collective-permute-start.15 = (bf16[2,8,256,1024]{3,2,0,1:T(8,128)(2,1)}, bf16[2,8,256,1024]{3,2,0,1:T(8,128)(2,1)S(1)}, u32[]{:S(2)}, u32[]{:S(2)}) collective-permute-start(bf16[2,8,256,1024]{3,2,0,1:T(8,128)(2,1)} %bitcast.164), channel_id=1, source_target_pairs={{0,8},{8,0},{1,9},{9,1},{2,10},{10,2},{3,11},{11,3},{4,12},{12,4},... | collective-permute-start | bytes 25165832 | tf_op jit(solution)/shard_map/ppermute | solution.py:87
  319.9 32.5 %slice-start.4 = ((s8[6291456]{0:T(1024)(128)(4,1)}), s8[2097152]{0:T(1024)(128)(4,1)S(1)}, s32[]{:S(2)}) async-start(s8[6291456]{0:T(1024)(128)(4,1)} %bitcast.154), calls=%async_computation.7 | async-start | bytes 4194304
  334.9 17.5 %slice-start.5 = ((s8[6291456]{0:T(1024)(128)(4,1)}), s8[4194304]{0:T(1024)(128)(4,1)S(1)}, s32[]{:S(2)}) async-start(s8[6291456]{0:T(1024)(128)(4,1)} %bitcast.154), calls=%async_computation.8 | async-start | bytes 8388608
  347.3 2.6 copy-start
  349.9 57.1 %slice-start.6 = ((s8[16777216]{0:T(1024)(128)(4,1)}), s8[4194304]{0:T(1024)(128)(4,1)S(1)}, s32[]{:S(2)}) async-start(s8[16777216]{0:T(1024)(128)(4,1)} %bitcast.161), calls=%async_computation.9 | async-start | bytes 8388608
  349.9 57.1 %slice-start.7 = ((s8[16777216]{0:T(1024)(128)(4,1)}), s8[4194304]{0:T(1024)(128)(4,1)S(1)}, s32[]{:S(2)}) async-start(s8[16777216]{0:T(1024)(128)(4,1)} %bitcast.161), calls=%async_computation.10 | async-start | bytes 8388608
  352.4 33.2 %collective-permute-start.10 = (bf16[768,512]{0,1:T(8,128)(2,1)}, bf16[768,512]{0,1:T(8,128)(2,1)S(1)}, u32[]{:S(2)}, u32[]{:S(2)}) collective-permute-start(bf16[768,512]{0,1:T(8,128)(2,1)} %get-tuple-element.25), channel_id=1, source_target_pairs={{0,3},{1,4},{2,5},{3,6},{4,7},{5,0},{6,1},{7,2},{8,11},{9,12},{10,... | collective-permute-start | bytes 2359304 | tf_op jit(solution)/shard_map/ppermute | solution.py:30
  352.4 37.5 %collective-permute-start.11 = (bf16[768,512]{0,1:T(8,128)(2,1)}, bf16[768,512]{0,1:T(8,128)(2,1)S(1)}, u32[]{:S(2)}, u32[]{:S(2)}) collective-permute-start(bf16[768,512]{0,1:T(8,128)(2,1)} %get-tuple-element.24), channel_id=1, source_target_pairs={{0,4},{1,5},{2,6},{3,7},{4,0},{5,1},{6,2},{7,3},{8,12},{9,13},{10,... | collective-permute-start | bytes 2359304 | tf_op jit(solution)/shard_map/ppermute | solution.py:30
  352.4 14.4 %copy-start.7 = (bf16[768,512]{0,1:T(8,128)(2,1)S(1)}, bf16[768,512]{0,1:T(8,128)(2,1)}, u32[]{:S(2)}) copy-start(bf16[768,512]{0,1:T(8,128)(2,1)} %get-tuple-element.21) | copy-start | bytes 2359300
  352.4 33.2 %copy-start.6 = (bf16[768,512]{0,1:T(8,128)(2,1)S(1)}, bf16[768,512]{0,1:T(8,128)(2,1)}, u32[]{:S(2)}) copy-start(bf16[768,512]{0,1:T(8,128)(2,1)} %get-tuple-element.20) | copy-start | bytes 2359300
  352.4 54.6 %slice-start.8 = ((s8[16777216]{0:T(1024)(128)(4,1)}), s8[4194304]{0:T(1024)(128)(4,1)S(1)}, s32[]{:S(2)}) async-start(s8[16777216]{0:T(1024)(128)(4,1)} %bitcast.161), calls=%async_computation.11 | async-start | bytes 8388608
  352.5 54.6 %slice-start.9 = ((s8[16777216]{0:T(1024)(128)(4,1)}), s8[4194304]{0:T(1024)(128)(4,1)S(1)}, s32[]{:S(2)}) async-start(s8[16777216]{0:T(1024)(128)(4,1)} %bitcast.161), calls=%async_computation.12 | async-start | bytes 8388608
  361.8 52.5 %collective-permute-start.12 = (bf16[768,512]{0,1:T(8,128)(2,1)}, bf16[768,512]{0,1:T(8,128)(2,1)}, u32[]{:S(2)}, u32[]{:S(2)}) collective-permute-start(bf16[768,512]{0,1:T(8,128)(2,1)} %get-tuple-element.23), channel_id=1, source_target_pairs={{0,5},{1,6},{2,7},{3,0},{4,1},{5,2},{6,3},{7,4},{8,13},{9,14},{10,... | collective-permute-start | bytes 2359304 | tf_op jit(solution)/shard_map/ppermute | solution.py:30
  365.0 55.7 %collective-permute-start.13 = (bf16[768,512]{0,1:T(8,128)(2,1)}, bf16[768,512]{0,1:T(8,128)(2,1)}, u32[]{:S(2)}, u32[]{:S(2)}) collective-permute-start(bf16[768,512]{0,1:T(8,128)(2,1)} %get-tuple-element.22), channel_id=1, source_target_pairs={{0,6},{1,7},{2,0},{3,1},{4,2},{5,3},{6,4},{7,5},{8,14},{9,15},{10,... | collective-permute-start | bytes 2359304 | tf_op jit(solution)/shard_map/ppermute | solution.py:30
  366.8 58.8 %collective-permute-start.14 = (bf16[768,512]{0,1:T(8,128)(2,1)S(1)}, bf16[768,512]{0,1:T(8,128)(2,1)}, u32[]{:S(2)}, u32[]{:S(2)}) collective-permute-start(bf16[768,512]{0,1:T(8,128)(2,1)S(1)} %copy-done.7), channel_id=1, source_target_pairs={{0,7},{1,0},{2,1},{3,2},{4,3},{5,4},{6,5},{7,6},{8,15},{9,8},{10,9... | collective-permute-start | bytes 2359304 | tf_op jit(solution)/shard_map/ppermute | solution.py:30
  385.6 60.2 %collective-permute-start.8 = (bf16[768,512]{0,1:T(8,128)(2,1)S(1)}, bf16[768,512]{0,1:T(8,128)(2,1)}, u32[]{:S(2)}, u32[]{:S(2)}) collective-permute-start(bf16[768,512]{0,1:T(8,128)(2,1)S(1)} %copy-done.6), channel_id=1, source_target_pairs={{0,1},{1,2},{2,3},{3,4},{4,5},{5,6},{6,7},{7,0},{8,9},{9,10},{10,1... | collective-permute-start | bytes 2359304 | tf_op jit(solution)/shard_map/ppermute | solution.py:30
  389.9 55.9 %collective-permute-start.9 = (bf16[768,512]{0,1:T(8,128)(2,1)S(1)}, bf16[768,512]{0,1:T(8,128)(2,1)}, u32[]{:S(2)}, u32[]{:S(2)}) collective-permute-start(bf16[768,512]{0,1:T(8,128)(2,1)S(1)} %get-tuple-element.26), channel_id=1, source_target_pairs={{0,2},{1,3},{2,4},{3,5},{4,6},{5,7},{6,0},{7,1},{8,10},{9,11},{10,... | collective-permute-start | bytes 2359304 | tf_op jit(solution)/shard_map/ppermute | solution.py:30
Sparse Core Ops, SparseCore 0:
  10.4 149.2 all-gather.2
  297.0 143.2 reduce-scatter.1

commit v4 on v2

--- a/solution.py
+++ b/solution.py
@@ -13,28 +13,59 @@
     return [(i, (i + k) % n) for i in range(n)]
 
 
-def gather_major(piece, axis_name):
+def in_order(rel, axis_name):
     n = lax.axis_size(axis_name)
     me = lax.axis_index(axis_name)
-    recv = [piece] + [lax.ppermute(piece, axis_name, ring_pairs(n, k)) for k in range(1, n)]
-    arr = jnp.stack([recv[(-m) % n] for m in range(n)] * 2, axis=0)
+    arr = jnp.stack(list(rel) * 2, axis=0)
     return lax.dynamic_slice_in_dim(arr, (n - me) % n, n, axis=0)
 
 
-def scatter_sum_major(full, axis_name):
+def ring_gather(x, axis_name):
+    n = lax.axis_size(axis_name)
+    if n == 2:
+        return in_order([x, lax.ppermute(x, axis_name, ring_pairs(n, 1))], axis_name)
+    if n == 4:
+        half = x.shape[0] // 2
+        from_prev = lax.ppermute(x, axis_name, ring_pairs(n, 1))
+        from_next = lax.ppermute(x, axis_name, ring_pairs(n, n - 1))
+        far_a = lax.ppermute(from_prev[:half], axis_name, ring_pairs(n, 1))
+        far_b = lax.ppermute(from_next[half:], axis_name, ring_pairs(n, n - 1))
+        far = jnp.concatenate([far_a, far_b], axis=0)
+        return in_order([x, from_next, far, from_prev], axis_name)
+    recv = [x] + [lax.ppermute(x, axis_name, ring_pairs(n, k)) for k in range(1, n)]
+    return in_order([recv[(-m) % n] for m in range(n)], axis_name)
+
+
+def ring_reduce(blocks, axis_name):
     n = lax.axis_size(axis_name)
     me = lax.axis_index(axis_name)
-    total = lax.dynamic_index_in_dim(full, me, axis=0, keepdims=False).astype(jnp.float32)
+
+    def blk(k):
+        return lax.dynamic_index_in_dim(blocks, (me + k) % n, axis=0, keepdims=False).astype(jnp.float32)
+
+    def send(v, k):
+        return lax.ppermute(v.astype(jnp.bfloat16), axis_name, ring_pairs(n, k)).astype(jnp.float32)
+
+    if n == 4:
+        far = blk(2)
+        half = far.shape[0] // 2
+        got_a = send(far[:half], 1)
+        got_b = send(far[half:], n - 1)
+        nxt = blk(1)
+        prv = blk(n - 1)
+        nxt = jnp.concatenate([nxt[:half] + got_a, nxt[half:]], axis=0)
+        prv = jnp.concatenate([prv[:half], prv[half:] + got_b], axis=0)
+        return blk(0) + send(nxt, 1) + send(prv, n - 1)
+    total = blk(0)
     for k in range(1, n):
-        piece = lax.dynamic_index_in_dim(full, (me + k) % n, axis=0, keepdims=False)
-        total = total + lax.ppermute(piece, axis_name, ring_pairs(n, k)).astype(jnp.float32)
-    return total.astype(jnp.bfloat16)
+        total = total + send(blk(k), k)
+    return total
 
 
 def local(hidden, combine_weight, down_weight, cotangent, expert_rows, block_expert, slot_token):
     slot_count, hidden_width = hidden.shape
     block_count = block_expert.shape[0]
-    n_dp = lax.axis_size("dp")
+    n_dp = lax.axis_size(("z", "xl"))
     part_width = cotangent.shape[1]
     positions = jnp.arange(slot_count, dtype=jnp.int32)
     blocks = positions // BLK
@@ -49,11 +80,15 @@
     slot_scale = combine_weight * live.astype(jnp.float32)
     slot_expert = jnp.repeat(block_expert, BLK)
 
-    panel = lax.all_gather(jnp.transpose(down_weight, (1, 0, 2)), "fsdp", axis=1, tiled=True)
-    model_width = panel.shape[1]
-    panel_parts = panel.reshape(EXPERTS, n_dp, part_width, hidden_width)
+    w = jnp.transpose(down_weight, (1, 0, 2))
+    w = ring_gather(w, "xh")
+    w = ring_gather(w, "y")
+    w = ring_gather(w, "core")
+    panel = jnp.transpose(w, (3, 2, 1, 0, 4, 5))
+    model_width = panel.shape[1] * panel.shape[2] * panel.shape[3] * panel.shape[4]
+    panel_parts = panel.reshape(EXPERTS, n_dp, model_width // n_dp, hidden_width)
 
-    full_cot = gather_major(cotangent, "dp")
+    full_cot = ring_gather(ring_gather(cotangent, "xl"), "z").reshape(n_dp, slot_count, part_width)
     tok_hot = (slot_token[:, None] == positions[None, :]).astype(jnp.bfloat16)
     picked = jnp.einsum("st,jtc->jsc", tok_hot, full_cot, preferred_element_type=jnp.float32)
     slot_cot = (slot_scale[None, :, None] * picked).astype(jnp.bfloat16)
@@ -74,11 +109,9 @@
             )
         )
     device_grad = jnp.stack(grads, axis=0)
-    device_grad, panel_parts = lax.optimization_barrier((device_grad, panel_parts))
-    summed = lax.psum_scatter(device_grad, "fsdp", scatter_dimension=1, tiled=True).astype(
-        jnp.float32
-    )
-    grad_scale = 1.0 / math.sqrt(lax.axis_size("fsdp") * slot_count)
+    fsdp = ("xh", "y", "core")
+    summed = lax.psum_scatter(device_grad, fsdp, scatter_dimension=1, tiled=True).astype(jnp.float32)
+    grad_scale = 1.0 / math.sqrt(lax.axis_size(fsdp) * slot_count)
     grad_down = jnp.transpose((summed * grad_scale).astype(jnp.bfloat16), (1, 0, 2))
 
     combined = None
@@ -93,7 +126,10 @@
         out_e = jnp.einsum("th,jch->jtc", hid_e, panel_parts[e], preferred_element_type=jnp.float32)
         term = scale_e[None, :, None] * out_e
         combined = term if combined is None else combined + term
-    expert_out = scatter_sum_major(combined.astype(jnp.bfloat16), "dp")
+    token_part = combined.astype(jnp.bfloat16)
+    n_xl = lax.axis_size("xl")
+    by_z = ring_reduce(token_part.reshape(n_dp // n_xl, n_xl, slot_count, part_width), "z")
+    expert_out = ring_reduce(by_z, "xl").astype(jnp.bfloat16)
 
     gh = []
     for e in range(EXPERTS):
@@ -111,14 +147,22 @@
 
 
 def solution(mesh):
+    n_core = 2
+    n_fsdp = mesh.shape["fsdp"]
+    n_dp = mesh.shape["dp"]
+    n_x = 2
+    shape = (n_x, n_fsdp // (n_x * n_core), n_core, n_dp // n_x, n_x)
+    fine = jax.sharding.Mesh(mesh.devices.reshape(shape), ("xh", "y", "core", "z", "xl"))
+    rows = ("xh", "y", "core")
+    cols = ("z", "xl")
     in_specs = (
-        P("fsdp", "dp"),
-        P("fsdp"),
-        P("fsdp", None, "dp"),
-        P("fsdp", "dp"),
-        P("fsdp", None),
-        P("fsdp"),
-        P("fsdp"),
+        P(rows, cols),
+        P(rows),
+        P(rows, None, cols),
+        P(rows, cols),
+        P(rows, None),
+        P(rows),
+        P(rows),
     )
-    out_specs = (P("fsdp", "dp"), P("fsdp", "dp"), P("fsdp", None, "dp"))
-    return jax.shard_map(local, mesh=mesh, in_specs=in_specs, out_specs=out_specs, check_vma=False)
+    out_specs = (P(rows, cols), P(rows, cols), P(rows, None, cols))
+    return jax.shard_map(local, mesh=fine, in_specs=in_specs, out_specs=out_specs, check_vma=False)

time: 395 us -> 478 us (1.21)
  other arithmetic: 25.2 us -> 126 us
  local copies, waits for them, and re-layouts: 63.4 us -> 146 us
  starting transfers between devices: 91.3 us -> 28 us
  waiting for transfers between devices: 126 us -> 83 us
    transpose x0 -> x1, other arithmetic: none -> 74.6 us  [local(): panel = jnp.transpose(w, (3, 2, 1, 0, 4, 5))]
    ppermute x14 -> x16, starting transfers between devices: 91.2 us -> 28 us  [the longest x3 7.63 us: ring_gather(): lax.ppermute(x, axis_name, ring_pairs(n, 1))]
    slice x0 -> x8, local copies, waits for them, and re-layouts: none -> 52.6 us  [the longest x3 43.8 us: local(): panel_parts[e]]
    reduce_scatter x1, waiting for transfers between devices: 26.3 us -> 0.01 us  [local(): lax.psum_scatter(device_grad, fsdp, scatter_dimension=1, tiled=True)]
    unnamed x42 -> x48, local copies, waits for them, and re-layouts: 12.6 us -> 36.4 us
    unnamed x2 -> x8, other arithmetic: 0.01 us -> 20.5 us
    all_gather x1 -> x0, local copies, waits for them, and re-layouts: 16.4 us -> none  [local(): lax.all_gather(jnp.transpose(down_weight, (1, 0, 2)), 'fsdp', axis=1, til...]
    ppermute x14 -> x16, waiting for transfers between devices: 98.5 us -> 82.9 us  [the longest x5 44.9 us: send(): lax.ppermute(v.astype(jnp.bfloat16), axis_name, ring_pairs(n, k))]
  transfers between devices with their start and end apart: 16 -> 17, of which waited for: 7 -> 8; matrix products, arithmetic and copies ran while one was open for 35% -> 67% of each run, Pallas kernels for 0% -> 0%
where the time goes in v4:
time: 478 us; the launch traced here: 469 us
  local copies, waits for them, and re-layouts  146 us (31%)
  other arithmetic  126 us (26%)
  waiting for transfers between devices  83 us (17%)
  matrix products  69.8 us (15%)
  starting transfers between devices  28 us (6%)
  between operations  16 us (3%)
    transpose x1, other arithmetic, local(): panel = jnp.transpose(w, (3, 2, 1, 0, 4, 5))  74.6 us
    ppermute x5, waiting for transfers between devices, send(): lax.ppermute(v.astype(jnp.bfloat16), axis_name, ring_pairs(n, k))  44.9 us
    slice x3, local copies, waits for them, and re-layouts, local(): panel_parts[e]  43.8 us
    unnamed x48, local copies, waits for them, and re-layouts  36.4 us
    dot_general x2, matrix products, local(): jnp.einsum('th,jch->jtc', hid_e, panel_parts[e], preferred_element_type=j...  30 us
    ppermute x3, waiting for transfers between devices, ring_gather(): lax.ppermute(x, axis_name, ring_pairs(n, 1))  21.9 us
    unnamed x8, other arithmetic  20.5 us
    dot_general x2, matrix products, local(): jnp.einsum('sd,sh->dh', cot_e, hidden[a:b], preferred_element_type=jnp.fl...  16.7 us
  transfers between devices with their start and end apart: 17, of which 8 were waited for; matrix products, arithmetic and copies ran while one was open for 67% of the time, Pallas kernels for 0%

profile of v4, /device:TPU:1, one launch (start us, length us, event | category | flops | bytes accessed | tf_op | source)
XLA Modules:
  0.0 469.1 jit_solution(5752379345021704774)
XLA Ops:
  7.2 3.7 collective-permute-start
  16.5 17.0 %collective-permute-done = bf16[2,256,1024]{2,0,1:T(2,128)(2,1)S(1)} collective-permute-done((bf16[2,256,1024]{2,0,1:T(2,128)(2,1)}, bf16[2,256,1024]{2,0,1:T(2,128)(2,1)S(1)}, u32[]{:S(2)}, u32[]{:S(2)}) %collective-permute-start) | collective-permute-done | bytes 1048608 | tf_op jit(solution)/shard_map/ppermute | solution.py:26
  33.5 9.4 %bitcast_dynamic-update-slice_fusion.4 = (bf16[8,2,2,256,1024]{4,2,3,1,0:T(2,128)(2,1)}, bf16[2,2,256,1024]{3,1,2,0:T(2,128)(2,1)}) fusion(s32[]{:T(128)S(6)} %select_n.148, bf16[1,2,256,1024]{3,1,2,0:T(2,128)(2,1)S(1)} %bitcast.136, bf16[1,2,256,1024]{3,1,2,0:T(2,128)(2,1)} %bitcast.135), kind=kLoop, calls=%fused_computation.53 | loop fusion | flops 8388607 | bytes 6291460
  42.9 3.1 collective-permute-start.1
  46.0 4.9 %collective-permute-done.11 = bf16[768,512]{1,0:T(8,128)(2,1)} collective-permute-done((bf16[768,512]{1,0:T(8,128)(2,1)}, bf16[768,512]{1,0:T(8,128)(2,1)}, u32[]{:S(2)}, u32[]{:S(2)}) %collective-permute-start.11) | collective-permute-done | bytes 786464 | tf_op jit(solution)/shard_map/ppermute | solution.py:26
  50.9 4.0 bitcast_dynamic-update-slice_fusion.10
  54.9 3.8 collective-permute-start.12
  58.8 3.4 scatter_custom_fusion.1
  62.2 3.7 scatter_custom_fusion
  65.9 3.4 scatter_custom_fusion.2
  69.3 3.4 scatter_custom_fusion.3
  72.7 3.2 gather_fusion.1
  75.9 3.2 gather_fusion
  79.3 11.8 %collective-permute-done.12 = bf16[2,768,512]{2,1,0:T(8,128)(2,1)} collective-permute-done((bf16[2,768,512]{2,1,0:T(8,128)(2,1)}, bf16[2,768,512]{2,1,0:T(8,128)(2,1)}, u32[]{:S(2)}, u32[]{:S(2)}) %collective-permute-start.12) | collective-permute-done | bytes 1572896 | tf_op jit(solution)/shard_map/ppermute | solution.py:30
  92.3 3.5 collective-permute-start.15
  101.7 2.8 collective-permute-start.4
  105.8 4.3 bitcast_dynamic-update-slice_fusion.2
  110.2 4.4 collective-permute-done.14
  115.8 3.5 bitcast_dynamic-update-slice_fusion.6
  119.3 3.4 bitcast_dynamic-update-slice_fusion.11
  122.7 2.7 bitcast_dynamic-update-slice_fusion.9
  126.7 2.7 bitcast_dynamic-update-slice_fusion.7
  133.3 3.2 bitcast_dynamic-update-slice_fusion.5
  136.4 3.2 bitcast_dynamic-update-slice_fusion.3
  143.7 8.0 %constant_dynamic-slice_fusion.8 = bf16[4,2,2,256,1024]{4,2,3,1,0:T(2,128)(2,1)} fusion(bf16[8,2,2,256,1024]{4,2,3,1,0:T(2,128)(2,1)S(1)} %bitcast_dynamic-update-slice_fusion.1, s32[]{:T(128)S(6)} %select_n.150), kind=kLoop, calls=%fused_computation.114 | loop fusion | bytes 16777220 | tf_op jit(solution)/shard_map/dynamic_slice | solution.py:20
  151.9 3.7 collective-permute-start.5
  155.5 3.5 constant_dynamic-slice_fusion.3
  159.0 7.5 %multiply_convert_fusion = bf16[8,512,768]{2,1,0:T(8,128)(2,1)} fusion(f32[768]{0:T(1024)S(1)} %get-tuple-element.11, bf16[8,768,512]{2,1,0:T(8,128)(2,1)S(1)} %bitcast.131, s32[768]{0:T(1024)S(1)} %copy-done.8), kind=kOutput, calls=%fused_computation.15 | convolution fusion | flops 4838719488 | bytes 12589056 | tf_op jit(solution)/shard_map/st,jtc->jsc/dot_general | solution.py:93
  166.5 9.3 %fusion.80 = (bf16[640,8,512]{0,2,1:T(8,128)(2,1)}, bf16[640,8,512]{0,2,1:T(8,128)(2,1)}) fusion(bf16[768,8,512]{0,2,1:T(8,128)(2,1)} %bitcast.118), kind=kLoop, calls=%fused_computation.145 | loop fusion | bytes 20971520 | tf_op jit(solution)/shard_map/slice | solution.py:104
  175.8 8.9 %bitcast_select_fusion = (bf16[640,4096]{0,1:T(8,128)(2,1)}, bf16[640,4096]{0,1:T(8,128)(2,1)}) fusion(bf16[640,8,512]{0,2,1:T(8,128)(2,1)} %get-tuple-element.18, pred[640]{0:T(1024)(128)(4,1)S(1)} %broadcast_bitcast_fusion, bf16[640,8,512]{0,2,1:T(8,128)(2,1)} %get-tuple-element.17, pred[640]{0:T(1024)(128)(4,1)S(1)} %broadcast_bitcast_fusion.1), kind=kLoop, calls=%fused_computation.23 | loop fusion | flops 5242880 | bytes 20972800 | tf_op jit(solution)/shard_map/jit(_where)/select_n | solution.py:105
  184.7 9.5 %convert_bitcast_fusion = bf16[1,4096,1024]{2,1,0:T(8,128)(2,1)S(1)} fusion(bf16[640,4096]{0,1:T(8,128)(2,1)} %get-tuple-element.33, bf16[768,1024]{1,0:T(8,128)(2,1)S(1)} %copy-done.11), kind=kOutput, calls=%fused_computation.17 | convolution fusion | flops 5372903424 | bytes 14942208 | tf_op jit(solution)/shard_map/sd,sh->dh/dot_general | solution.py:107
  194.3 7.2 %convert_bitcast_fusion.1 = bf16[1,4096,1024]{2,1,0:T(8,128)(2,1)S(1)} fusion(bf16[640,4096]{0,1:T(8,128)(2,1)S(1)} %copy-done.3, bf16[768,1024]{1,0:T(8,128)(2,1)S(1)} %copy-done.11), kind=kOutput, calls=%fused_computation.18 | convolution fusion | flops 5372903424 | bytes 14942208 | tf_op jit(solution)/shard_map/sd,sh->dh/dot_general | solution.py:107
  201.5 6.7 %pad_maximum_fusion = bf16[2,4096,1024]{2,1,0:T(8,128)(2,1)} fusion(bf16[1,4096,1024]{2,1,0:T(8,128)(2,1)S(1)} %convert_bitcast_fusion, bf16[1,4096,1024]{2,1,0:T(8,128)(2,1)S(1)} %convert_bitcast_fusion.1), kind=kLoop, calls=%fused_computation.13 | loop fusion | flops 8388608 | bytes 33554432 | tf_op jit(solution)/shard_map/stack | solution.py:111
  208.2 8.2 %fusion.91 = bf16[1,4,2,2,256,1024]{5,3,4,2,1,0:T(2,128)(2,1)} fusion(bf16[8,2,2,256,1024]{4,2,3,1,0:T(2,128)(2,1)} %copy-done.2, s32[]{:T(128)S(6)} %select_n.150), kind=kLoop, calls=%fused_computation.147 | loop fusion | bytes 16777220 | tf_op jit(solution)/shard_map/stack | solution.py:19
  216.4 74.6 %fusion.3 = bf16[2,2,4,2,256,1024]{5,0,4,1,2,3:T(2,128)(2,1)S(1)} fusion(s32[]{:T(128)S(6)} %select_n.152, bf16[1,4,2,2,256,1024]{5,3,4,2,1,0:T(2,128)(2,1)} %bitcast.11, bf16[1,4,2,2,256,1024]{5,3,4,2,1,0:T(2,128)(2,1)} %fusion.91), kind=kLoop, calls=%fused_computation.14 | loop fusion | flops 25165824 | bytes 33554436 | tf_op jit(solution)/shard_map/transpose | solution.py:87
  291.0 25.6 %fusion.79 = (bf16[1,2,4,2,256,1024]{5,0,4,1,2,3:T(2,128)(2,1)}, bf16[1,2,4,2,256,1024]{5,0,4,1,2,3:T(2,128)(2,1)}) fusion(bf16[2,2,4,2,256,1024]{5,0,4,1,2,3:T(2,128)(2,1)S(1)} %fusion.3), kind=kLoop, calls=%fused_computation.144 | loop fusion | bytes 33554432 | tf_op jit(solution)/shard_map/slice | solution.py:126
  316.6 13.1 %copy.20 = bf16[1,2,4,2,256,1024]{5,4,3,2,1,0:T(8,128)(2,1)} copy(bf16[1,2,4,2,256,1024]{5,0,4,1,2,3:T(2,128)(2,1)} %get-tuple-element.16) | data formatting | bytes 16777216 | tf_op jit(solution)/shard_map/slice | solution.py:126
  331.0 5.2 %copy.21 = bf16[1,2,4,2,256,1024]{5,4,3,2,1,0:T(8,128)(2,1)} copy(bf16[1,2,4,2,256,1024]{5,0,4,1,2,3:T(2,128)(2,1)S(1)} %copy-done) | data formatting | bytes 16777216 | tf_op jit(solution)/shard_map/slice | solution.py:126
  336.2 14.3 %fusion.40 = f32[8,512,768]{2,1,0:T(8,128)} fusion(bf16[8,512,1024]{2,1,0:T(8,128)(2,1)} %bitcast.123, bf16[768,1024]{1,0:T(8,128)(2,1)S(1)} %copy-done.11, s32[768]{0:T(1024)S(1)} %scatter_custom_fusion.1, pred[768]{0:T(1024)(128)(4,1)S(1)} %scatter_custom_fusion), kind=kOutput, calls=%fused_computation.80 | convolution fusion | flops 7652376576 | bytes 22548224 | tf_op jit(solution)/shard_map/th,jch->jtc/dot_general | solution.py:126
  350.5 15.7 %add_convert_fusion = bf16[8,512,768]{2,1,0:T(8,128)(2,1)} fusion(f32[8,512,768]{2,1,0:T(8,128)} %fusion.40, f32[768]{0:T(1024)S(1)} %broadcast_select_fusion, f32[768]{0:T(1024)S(1)} %broadcast_select_fusion.1, bf16[8,512,1024]{2,1,0:T(8,128)(2,1)} %bitcast.127, bf16[768,1024]{1,0:T(8,128)(2,1)S(1)} %copy-done.11, s32[768]{0:T(1024)S(1)} %copy-done.7, ...), kind=kOutput, calls=%fused_computation.16 | convolution fusion | flops 7664959488 | bytes 28845824 | tf_op jit(solution)/shard_map/th,jch->jtc/dot_general | solution.py:126
  366.2 3.8 constant_dynamic-slice_fusion
  379.6 12.1 %collective-permute-done.8 = bf16[1,768,512]{2,1,0:T(8,128)(2,1)} collective-permute-done((bf16[1,768,512]{2,1,0:T(8,128)(2,1)}, bf16[1,768,512]{2,1,0:T(8,128)(2,1)}, u32[]{:S(2)}, u32[]{:S(2)}) %collective-permute-start.8) | collective-permute-done | bytes 786464 | tf_op jit(solution)/shard_map/ppermute | solution.py:47
  395.5 3.2 collective-permute-start.9
  403.6 9.7 %fusion.24 = bf16[640,1024]{1,0:T(8,128)(2,1)S(1)} fusion(bf16[8,512,1024]{2,1,0:T(8,128)(2,1)} %bitcast.128, bf16[8,768,512]{1,2,0:T(8,128)(2,1)} %bitcast.119), kind=kOutput, calls=%fused_computation.57 | convolution fusion | flops 5368709120 | bytes 14942208 | tf_op jit(solution)/shard_map/jsc,jch->sh/dot_general | solution.py:138
  413.3 18.5 %collective-permute-done.9 = bf16[2,768,512]{2,1,0:T(8,128)(2,1)} collective-permute-done((bf16[2,768,512]{2,1,0:T(8,128)(2,1)}, bf16[2,768,512]{2,1,0:T(8,128)(2,1)}, u32[]{:S(2)}, u32[]{:S(2)}) %collective-permute-start.9) | collective-permute-done | bytes 1572896 | tf_op jit(solution)/shard_map/ppermute | solution.py:47
  431.8 5.8 %collective-permute-done.7 = bf16[2,768,512]{2,1,0:T(8,128)(2,1)} collective-permute-done((bf16[2,768,512]{2,1,0:T(8,128)(2,1)}, bf16[2,768,512]{2,1,0:T(8,128)(2,1)}, u32[]{:S(2)}, u32[]{:S(2)}) %collective-permute-start.7) | collective-permute-done | bytes 1572896 | tf_op jit(solution)/shard_map/ppermute | solution.py:47
  441.6 5.8 %fusion.21 = bf16[640,1024]{1,0:T(8,128)(2,1)S(1)} fusion(bf16[8,512,1024]{2,1,0:T(8,128)(2,1)S(1)} %bitcast.126, bf16[8,768,512]{1,2,0:T(8,128)(2,1)S(1)} %bitcast.122), kind=kOutput, calls=%fused_computation.56 | convolution fusion | flops 5368709120 | bytes 14942208 | tf_op jit(solution)/shard_map/jsc,jch->sh/dot_general | solution.py:138
  448.9 8.6 %collective-permute-done.10 = bf16[768,512]{1,0:T(8,128)(2,1)S(1)} collective-permute-done((bf16[768,512]{1,0:T(8,128)(2,1)S(1)}, bf16[768,512]{1,0:T(8,128)(2,1)S(1)}, u32[]{:S(2)}, u32[]{:S(2)}) %collective-permute-start.10) | collective-permute-done | bytes 786464 | tf_op jit(solution)/shard_map/ppermute | solution.py:47
  (103 shorter events, 53.4 us)
Async XLA Ops:
  7.2 43.8 %copy-start.5 = (bf16[768,512]{1,0:T(8,128)(2,1)S(1)}, bf16[768,512]{1,0:T(8,128)(2,1)}, u32[]{:S(2)}) copy-start(bf16[768,512]{1,0:T(8,128)(2,1)} %param.10) | copy-start | bytes 2359300
  7.2 451.4 %reduce-scatter.2.cloned.1.call-start = ((), (), s32[]{:S(2)}) async-start(), calls=%async_computation.1 | async-start | bytes 17825792 | tf_op jit(solution)/shard_map/reduce_scatter | solution.py:113
  7.2 26.3 %collective-permute-start = (bf16[2,256,1024]{2,0,1:T(2,128)(2,1)}, bf16[2,256,1024]{2,0,1:T(2,128)(2,1)S(1)}, u32[]{:S(2)}, u32[]{:S(2)}) collective-permute-start(bf16[2,256,1024]{2,0,1:T(2,128)(2,1)} %bitcast.134), channel_id=1, source_target_pairs={{0,64},{64,0},{1,65},{65,1},{2,66},{66,2},{3,67},{67,3},{4,68},{68... | collective-permute-start | bytes 3145736 | tf_op jit(solution)/shard_map/ppermute | solution.py:26
  10.9 40.0 %collective-permute-start.11 = (bf16[768,512]{1,0:T(8,128)(2,1)}, bf16[768,512]{1,0:T(8,128)(2,1)}, u32[]{:S(2)}, u32[]{:S(2)}) collective-permute-start(bf16[768,512]{1,0:T(8,128)(2,1)} %param.10), channel_id=1, source_target_pairs={{0,1},{1,0},{2,3},{3,2},{4,5},{5,4},{6,7},{7,6},{8,9},{9,8},{10,11... | collective-permute-start | bytes 2359304 | tf_op jit(solution)/shard_map/ppermute | solution.py:26
  14.5 64.7 %copy-start.9 = (pred[6]{0:T(512)(128)(4,1)}, pred[6]{0:T(512)(128)(4,1)S(1)}, u32[]{:S(2)}) copy-start(pred[6]{0:T(512)(128)(4,1)S(1)} %get-tuple-element.28) | copy-start | bytes 22
  33.5 25.3 %copy-start.8 = (s32[768]{0:T(1024)S(1)}, s32[768]{0:T(1024)}, u32[]{:S(2)}) copy-start(s32[768]{0:T(1024)} %param.13) | copy-start | bytes 9220
  42.9 56.8 %collective-permute-start.1 = (bf16[2,2,256,1024]{3,1,2,0:T(2,128)(2,1)}, bf16[2,2,256,1024]{3,1,2,0:T(2,128)(2,1)}, u32[]{:S(2)}, u32[]{:S(2)}) collective-permute-start(bf16[2,2,256,1024]{3,1,2,0:T(2,128)(2,1)} %get-tuple-element.14), channel_id=1, source_target_pairs={{0,48},{16,0},{32,16},{48,32},{1,49},{17,1},{33,17},{49,33},{2,50}... | collective-permute-start | bytes 6291464 | tf_op jit(solution)/shard_map/ppermute | solution.py:30
  46.0 58.5 %collective-permute-start.2 = (bf16[2,2,256,1024]{3,1,2,0:T(2,128)(2,1)}, bf16[2,2,256,1024]{3,1,2,0:T(2,128)(2,1)S(1)}, u32[]{:S(2)}, u32[]{:S(2)}) collective-permute-start(bf16[2,2,256,1024]{3,1,2,0:T(2,128)(2,1)} %get-tuple-element.14), channel_id=1, source_target_pairs={{0,16},{16,32},{32,48},{48,0},{1,17},{17,33},{33,49},{49,1},{2,18}... | collective-permute-start | bytes 6291464 | tf_op jit(solution)/shard_map/ppermute | solution.py:29
  54.9 36.2 %collective-permute-start.12 = (bf16[2,768,512]{2,1,0:T(8,128)(2,1)}, bf16[2,768,512]{2,1,0:T(8,128)(2,1)}, u32[]{:S(2)}, u32[]{:S(2)}) collective-permute-start(bf16[2,768,512]{2,1,0:T(8,128)(2,1)} %get-tuple-element.10), channel_id=1, source_target_pairs={{0,6},{2,0},{4,2},{6,4},{1,7},{3,1},{5,3},{7,5},{8,14},{10,8},{12,... | collective-permute-start | bytes 4718600 | tf_op jit(solution)/shard_map/ppermute | solution.py:30
  58.7 37.1 %collective-permute-start.13 = (bf16[2,768,512]{2,1,0:T(8,128)(2,1)}, bf16[2,768,512]{2,1,0:T(8,128)(2,1)}, u32[]{:S(2)}, u32[]{:S(2)}) collective-permute-start(bf16[2,768,512]{2,1,0:T(8,128)(2,1)} %get-tuple-element.10), channel_id=1, source_target_pairs={{0,2},{2,4},{4,6},{6,0},{1,3},{3,5},{5,7},{7,1},{8,10},{10,12},{12... | collective-permute-start | bytes 4718600 | tf_op jit(solution)/shard_map/ppermute | solution.py:29
  72.7 6.4 %copy-start.6 = (s32[768]{0:T(1024)}, s32[768]{0:T(1024)S(1)}, u32[]{:S(2)}) copy-start(s32[768]{0:T(1024)S(1)} %scatter_custom_fusion.3) | copy-start | bytes 9220
  92.3 17.8 %collective-permute-start.15 = (bf16[1,768,512]{2,1,0:T(8,128)(2,1)S(1)}, bf16[1,768,512]{2,1,0:T(8,128)(2,1)S(1)}, u32[]{:S(2)}, u32[]{:S(2)}) collective-permute-start(bf16[1,768,512]{2,1,0:T(8,128)(2,1)S(1)} %slice.182), channel_id=1, source_target_pairs={{0,6},{2,0},{4,2},{6,4},{1,7},{3,1},{5,3},{7,5},{8,14},{10,8},{12,... | collective-permute-start | bytes 2359304 | tf_op jit(solution)/shard_map/ppermute | solution.py:32
  97.0 17.6 %collective-permute-start.14 = (bf16[1,768,512]{2,1,0:T(8,128)(2,1)S(1)}, bf16[1,768,512]{2,1,0:T(8,128)(2,1)S(1)}, u32[]{:S(2)}, u32[]{:S(2)}) collective-permute-start(bf16[1,768,512]{2,1,0:T(8,128)(2,1)S(1)} %slice.181), channel_id=1, source_target_pairs={{0,2},{2,4},{4,6},{6,0},{1,3},{3,5},{5,7},{7,1},{8,10},{10,12},{12... | collective-permute-start | bytes 2359304 | tf_op jit(solution)/shard_map/ppermute | solution.py:31
  101.7 27.7 %collective-permute-start.4 = (bf16[1,2,256,1024]{3,1,2,0:T(2,128)(2,1)S(1)}, bf16[1,2,256,1024]{3,1,2,0:T(2,128)(2,1)S(1)}, u32[]{:S(2)}, u32[]{:S(2)}) collective-permute-start(bf16[1,2,256,1024]{3,1,2,0:T(2,128)(2,1)S(1)} %slice.178), channel_id=1, source_target_pairs={{0,48},{16,0},{32,16},{48,32},{1,49},{17,1},{33,17},{49,33},{2,50}... | collective-permute-start | bytes 3145736 | tf_op jit(solution)/shard_map/ppermute | solution.py:32
  105.2 24.2 %collective-permute-start.3 = (bf16[1,2,256,1024]{3,1,2,0:T(2,128)(2,1)S(1)}, bf16[1,2,256,1024]{3,1,2,0:T(2,128)(2,1)S(1)}, u32[]{:S(2)}, u32[]{:S(2)}) collective-permute-start(bf16[1,2,256,1024]{3,1,2,0:T(2,128)(2,1)S(1)} %slice.177), channel_id=1, source_target_pairs={{0,16},{16,32},{32,48},{48,0},{1,17},{17,33},{33,49},{49,1},{2,18}... | collective-permute-start | bytes 3145736 | tf_op jit(solution)/shard_map/ppermute | solution.py:31
  114.6 14.8 %copy-start.1 = (bf16[8,2,2,256,1024]{4,2,3,1,0:T(2,128)(2,1)S(1)}, bf16[8,2,2,256,1024]{4,2,3,1,0:T(2,128)(2,1)}, u32[]{:S(2)}) copy-start(bf16[8,2,2,256,1024]{4,2,3,1,0:T(2,128)(2,1)} %bitcast_dynamic-update-slice_fusion.2) | copy-start | bytes 50331652
  143.7 8.2 %copy-start.2 = (bf16[8,2,2,256,1024]{4,2,3,1,0:T(2,128)(2,1)}, bf16[8,2,2,256,1024]{4,2,3,1,0:T(2,128)(2,1)S(1)}, u32[]{:S(2)}) copy-start(bf16[8,2,2,256,1024]{4,2,3,1,0:T(2,128)(2,1)S(1)} %bitcast_dynamic-update-slice_fusion.1) | copy-start | bytes 50331652
  151.9 64.5 %collective-permute-start.5 = (bf16[4,2,2,256,1024]{4,2,3,1,0:T(2,128)(2,1)}, bf16[4,2,2,256,1024]{4,2,3,1,0:T(2,128)(2,1)}, u32[]{:S(2)}, u32[]{:S(2)}) collective-permute-start(bf16[4,2,2,256,1024]{4,2,3,1,0:T(2,128)(2,1)} %constant_dynamic-slice_fusion.8), channel_id=1, source_target_pairs={{0,8},{8,0},{1,9},{9,1},{2,10},{10,2},{3,11},{11,3},{4,12},{12,4},... | collective-permute-start | bytes 25165832 | tf_op jit(solution)/shard_map/ppermute | solution.py:26
  175.8 8.9 %copy-start.11 = (bf16[768,1024]{1,0:T(8,128)(2,1)S(1)}, bf16[768,1024]{1,0:T(8,128)(2,1)}, u32[]{:S(2)}) copy-start(bf16[768,1024]{1,0:T(8,128)(2,1)} %param.7) | copy-start | bytes 4718596
  184.7 9.6 %copy-start.3 = (bf16[640,4096]{0,1:T(8,128)(2,1)S(1)}, bf16[640,4096]{0,1:T(8,128)(2,1)}, u32[]{:S(2)}) copy-start(bf16[640,4096]{0,1:T(8,128)(2,1)} %get-tuple-element.34) | copy-start | bytes 15728644
  316.6 14.4 %copy-start = (bf16[1,2,4,2,256,1024]{5,0,4,1,2,3:T(2,128)(2,1)S(1)}, bf16[1,2,4,2,256,1024]{5,0,4,1,2,3:T(2,128)(2,1)}, u32[]{:S(2)}) copy-start(bf16[1,2,4,2,256,1024]{5,0,4,1,2,3:T(2,128)(2,1)} %get-tuple-element.15) | copy-start | bytes 25165828
  336.2 14.3 %copy-start.7 = (s32[768]{0:T(1024)S(1)}, s32[768]{0:T(1024)}, u32[]{:S(2)}) copy-start(s32[768]{0:T(1024)} %copy-done.6) | copy-start | bytes 9220
  366.2 10.4 %copy-start.10 = (pred[6]{0:T(512)(128)(4,1)S(1)}, pred[6]{0:T(512)(128)(4,1)}, u32[]{:S(2)}) copy-start(pred[6]{0:T(512)(128)(4,1)} %copy-done.9) | copy-start | bytes 22
  372.3 19.4 %collective-permute-start.8 = (bf16[1,768,512]{2,1,0:T(8,128)(2,1)}, bf16[1,768,512]{2,1,0:T(8,128)(2,1)}, u32[]{:S(2)}, u32[]{:S(2)}) collective-permute-start(bf16[1,768,512]{2,1,0:T(8,128)(2,1)} %bitcast.139), channel_id=1, source_target_pairs={{0,6},{2,0},{4,2},{6,4},{1,7},{3,1},{5,3},{7,5},{8,14},{10,8},{12,... | collective-permute-start | bytes 2359304 | tf_op jit(solution)/shard_map/ppermute | solution.py:47
  376.6 22.1 %collective-permute-start.6 = (bf16[1,768,512]{2,1,0:T(8,128)(2,1)}, bf16[1,768,512]{2,1,0:T(8,128)(2,1)}, u32[]{:S(2)}, u32[]{:S(2)}) collective-permute-start(bf16[1,768,512]{2,1,0:T(8,128)(2,1)} %bitcast.138), channel_id=1, source_target_pairs={{0,2},{2,4},{4,6},{6,0},{1,3},{3,5},{5,7},{7,1},{8,10},{10,12},{12... | collective-permute-start | bytes 2359304 | tf_op jit(solution)/shard_map/ppermute | solution.py:47
  377.9 13.8 %copy-start.4 = (bf16[1,1,768,512]{3,2,1,0:T(8,128)(2,1)S(1)}, bf16[1,1,768,512]{3,2,1,0:T(8,128)(2,1)}, u32[]{:S(2)}) copy-start(bf16[1,1,768,512]{3,2,1,0:T(8,128)(2,1)} %copy.40) | copy-start | bytes 2359300
  395.5 36.3 %collective-permute-start.9 = (bf16[2,768,512]{2,1,0:T(8,128)(2,1)}, bf16[2,768,512]{2,1,0:T(8,128)(2,1)}, u32[]{:S(2)}, u32[]{:S(2)}) collective-permute-start(bf16[2,768,512]{2,1,0:T(8,128)(2,1)} %pad_maximum_fusion.2), channel_id=1, source_target_pairs={{0,6},{2,0},{4,2},{6,4},{1,7},{3,1},{5,3},{7,5},{8,14},{10,8},{12,... | collective-permute-start | bytes 4718600 | tf_op jit(solution)/shard_map/ppermute | solution.py:47
  401.3 36.3 %collective-permute-start.7 = (bf16[2,768,512]{2,1,0:T(8,128)(2,1)}, bf16[2,768,512]{2,1,0:T(8,128)(2,1)}, u32[]{:S(2)}, u32[]{:S(2)}) collective-permute-start(bf16[2,768,512]{2,1,0:T(8,128)(2,1)} %pad_maximum_fusion.1), channel_id=1, source_target_pairs={{0,2},{2,4},{4,6},{6,0},{1,3},{3,5},{5,7},{7,1},{8,10},{10,12},{12... | collective-permute-start | bytes 4718600 | tf_op jit(solution)/shard_map/ppermute | solution.py:47
  403.6 38.0 %slice-start = ((s8[6291456]{0:T(1024)(128)(4,1)}), s8[4194304]{0:T(1024)(128)(4,1)S(1)}, s32[]{:S(2)}) async-start(s8[6291456]{0:T(1024)(128)(4,1)} %bitcast.120), calls=%async_computation.2 | async-start | bytes 8388608
  403.6 38.0 %slice-start.2 = ((s8[8388608]{0:T(1024)(128)(4,1)}), s8[4194304]{0:T(1024)(128)(4,1)S(1)}, s32[]{:S(2)}) async-start(s8[8388608]{0:T(1024)(128)(4,1)} %bitcast.124), calls=%async_computation.4 | async-start | bytes 8388608
  403.6 38.0 %slice-start.1 = ((s8[6291456]{0:T(1024)(128)(4,1)}), s8[2097152]{0:T(1024)(128)(4,1)S(1)}, s32[]{:S(2)}) async-start(s8[6291456]{0:T(1024)(128)(4,1)} %bitcast.120), calls=%async_computation.3 | async-start | bytes 4194304
  403.6 38.0 %slice-start.3 = ((s8[8388608]{0:T(1024)(128)(4,1)}), s8[4194304]{0:T(1024)(128)(4,1)S(1)}, s32[]{:S(2)}) async-start(s8[8388608]{0:T(1024)(128)(4,1)} %bitcast.124), calls=%async_computation.5 | async-start | bytes 8388608
  440.2 17.2 %collective-permute-start.10 = (bf16[768,512]{1,0:T(8,128)(2,1)S(1)}, bf16[768,512]{1,0:T(8,128)(2,1)S(1)}, u32[]{:S(2)}, u32[]{:S(2)}) collective-permute-start(bf16[768,512]{1,0:T(8,128)(2,1)S(1)} %fusion.52), channel_id=1, source_target_pairs={{0,1},{1,0},{2,3},{3,2},{4,5},{5,4},{6,7},{7,6},{8,9},{9,8},{10,11... | collective-permute-start | bytes 2359304 | tf_op jit(solution)/shard_map/ppermute | solution.py:47
Sparse Core Ops, SparseCore 0:
  208.3 143.4 reduce-scatter.1
